TPU v7x, 512 devices: a whole 4x8x8 slice. The times are simulated.
512 devices in a mesh: head: 16 (over y, core), seq: 32 (over z, x).
Axes of the slice: x: 4, y: 8, z: 8, core: 2. Of those that a mesh axis runs over, the one named last changes fastest.
Arguments:
- queries: bfloat16 [32768, 2048], P(('seq', 'head'))
- keys: bfloat16 [32768, 2048], P(('seq', 'head'))
- values: bfloat16 [32768, 2048], P(('seq', 'head')), may hold values from -6 to 6
- grad_out: bfloat16 [32768, 2048], P(('seq', 'head')), may hold values from -6 to 6
- random_blocks: int32 [256, 3], P('seq'), may hold values from 0 to 255, as said below
Outputs:
- attended: bfloat16 [32768, 2048], P(('seq', 'head'))
- grad_queries: bfloat16 [32768, 2048], P(('seq', 'head'))
- grad_keys: bfloat16 [32768, 2048], P(('seq', 'head'))
- grad_values: bfloat16 [32768, 2048], P(('seq', 'head'))
Inputs may be any that keep to these rules, and one draw needn't show every extreme that they name: `random_blocks`: within the rows of one sequence group (8 consecutive query blocks), at most 2 entries name blocks of any one group's range of 8 blocks, and in every group's rows one group's range is named exactly 2 times.
All inputs are finite; a program needn't handle non-finite values.
Results may differ from a plain program's by a relative error of at most 0.022.
Values may be sent and summed in bfloat16 or wider, within the bound.
No kernel may reach another device: no remote copies, remote signals or barrier semaphores. Data moves between devices by JAX's collectives and lax.ppermute only.
A program may use at most 192 MiB of HBM per device.

v0:
```python
import jax
import jax.numpy as jnp
from jax import lax
from jax.sharding import PartitionSpec as P

HD = 128
BLK = 128
RAND = 3


def with_halo(cells, sides, width):
    for axis, dim in sides:
        count = lax.axis_size(axis)
        ends = count - 1
        head = lax.slice_in_dim(cells, 0, width, axis=dim)
        tail = lax.slice_in_dim(cells, cells.shape[dim] - width, cells.shape[dim], axis=dim)
        cells = jnp.concatenate(
            [
                lax.ppermute(tail, axis, [(i, (i + 1) % count) for i in range(ends)]),
                cells,
                lax.ppermute(head, axis, [((i + 1) % count, i) for i in range(ends)]),
            ],
            axis=dim,
        )
    return cells


def broadcast(value, axis, source):
    kept = jnp.where(lax.axis_index(axis) == source, value, 0).astype(value.dtype)
    return lax.psum(kept, axis)


def slot_places(owners, groups, capacity):
    owner_hits = (owners[:, None] == jnp.arange(groups, dtype=jnp.int32)[None, :]).astype(jnp.int32)
    earlier = jnp.cumsum(owner_hits, axis=0) - owner_hits
    return owners * capacity + jnp.sum(earlier * owner_hits, axis=1)


def request_table(list_rows, query_count, groups, capacity):
    flat_rows = list_rows.reshape(-1)
    places = slot_places(flat_rows // query_count, groups, capacity)
    matches = places[None, :] == jnp.arange(groups * capacity, dtype=jnp.int32)[:, None]
    table = jnp.sum(jnp.where(matches, (flat_rows % query_count)[None, :], 0), axis=1)
    return table.reshape(groups, capacity)


def window_valid(my_group, query_count, groups):
    block_ids = jnp.arange(query_count, dtype=jnp.int32)
    left_ok = jnp.logical_not(jnp.logical_and(my_group == 0, block_ids == 0))
    right_ok = jnp.logical_not(
        jnp.logical_and(my_group == groups - 1, block_ids == query_count - 1)
    )
    all_true = jnp.ones((query_count, BLK), dtype=bool)
    return jnp.concatenate(
        [
            all_true,
            all_true,
            left_ok[:, None] & all_true,
            all_true,
            right_ok[:, None] & all_true,
            jnp.ones((query_count, RAND * BLK), dtype=bool),
        ],
        axis=1,
    )


def against_keys(rows, global_part, window_part, remote_part):
    return jnp.concatenate(
        [
            jnp.einsum("qihd,jhd->qhij", rows, global_part, preferred_element_type=jnp.float32),
            jnp.einsum("qihd,qjhd->qhij", rows, window_part, preferred_element_type=jnp.float32),
            jnp.einsum("qihd,qjhd->qhij", rows, remote_part, preferred_element_type=jnp.float32),
        ],
        axis=-1,
    )


def split_keys(table):
    return (table[..., : 2 * BLK], table[..., 2 * BLK : 5 * BLK], table[..., 5 * BLK :])


def weigh_keys(table, global_part, window_part, remote_part):
    global_w, window_w, random_w = split_keys(table)
    return (
        jnp.einsum("qhij,jhd->qihd", global_w, global_part, preferred_element_type=jnp.float32)
        + jnp.einsum("qhij,qjhd->qihd", window_w, window_part, preferred_element_type=jnp.float32)
        + jnp.einsum("qhij,qjhd->qihd", random_w, remote_part, preferred_element_type=jnp.float32)
    )


def key_terms(table, rows):
    global_w, window_w, random_w = split_keys(table)
    return (
        jnp.einsum("qhij,qihd->jhd", global_w, rows, preferred_element_type=jnp.float32),
        jnp.einsum("qhij,qihd->qjhd", window_w, rows, preferred_element_type=jnp.float32),
        jnp.einsum("qhij,qihd->qjhd", random_w, rows, preferred_element_type=jnp.float32),
    )


def shards(queries, keys, values, grad_out, random_blocks):
    groups = lax.axis_size("seq")
    my_group = lax.axis_index("seq")
    head_q, head_k, head_v, head_g = (
        lax.all_to_all(queries, "head", split_axis=1, concat_axis=0, tiled=True),
        lax.all_to_all(keys, "head", split_axis=1, concat_axis=0, tiled=True),
        lax.all_to_all(values, "head", split_axis=1, concat_axis=0, tiled=True),
        lax.all_to_all(grad_out, "head", split_axis=1, concat_axis=0, tiled=True),
    )
    group_tokens = head_q.shape[0]
    head_count = head_q.shape[1] // HD
    query_count = group_tokens // BLK
    capacity = max(2, 3 * query_count * RAND // (2 * groups))
    score_scale = HD ** (-0.5)
    key_value = jnp.stack([head_k, head_v])
    kv_blocks = key_value.reshape(2, query_count, BLK, head_count, HD)
    edged = with_halo(key_value, (("seq", 1),), BLK)
    edged = edged.reshape(2, query_count + 2, BLK, head_count, HD)
    window_kv = jnp.concatenate(
        [edged[:, 0:query_count], edged[:, 1 : query_count + 1], edged[:, 2 : query_count + 2]],
        axis=2,
    )
    global_kv = broadcast(kv_blocks[:, 0:2].reshape(2, 2 * BLK, head_count, HD), "seq", 0)
    flat_ids = random_blocks.reshape(-1)
    places = slot_places(flat_ids // query_count, groups, capacity)
    wanted = lax.all_to_all(
        request_table(random_blocks, query_count, groups, capacity),
        "seq",
        split_axis=0,
        concat_axis=0,
        tiled=True,
    )
    served = jnp.take(kv_blocks, wanted.reshape(-1), axis=1)
    served = served.reshape(2, groups, capacity, BLK, head_count, HD)
    fetched = lax.all_to_all(served, "seq", split_axis=1, concat_axis=1, tiled=True)
    chosen = jnp.take(fetched.reshape(2, groups * capacity, BLK, head_count, HD), places, axis=1)
    remote_kv = chosen.reshape(2, query_count, RAND * BLK, head_count, HD)
    query_blocks = head_q.reshape(query_count, BLK, head_count, HD)
    grad_blocks = head_g.reshape(query_count, BLK, head_count, HD)
    scores = score_scale * against_keys(query_blocks, global_kv[0], window_kv[0], remote_kv[0])
    valid = window_valid(my_group, query_count, groups)
    scores = jnp.where(valid[:, None, None, :], scores, -jnp.inf)
    row_max = jnp.max(scores, axis=-1, keepdims=True)
    exponent = jnp.exp(scores - row_max)
    attention_probs = exponent / jnp.sum(exponent, axis=-1, keepdims=True)
    weights = attention_probs.astype(jnp.bfloat16)
    attended = weigh_keys(weights, global_kv[1], window_kv[1], remote_kv[1]).astype(jnp.bfloat16)
    grad_prob = against_keys(grad_blocks, global_kv[1], window_kv[1], remote_kv[1])
    row_delta = jnp.sum(attention_probs * grad_prob, axis=-1, keepdims=True)
    grad_score = (score_scale * attention_probs * (grad_prob - row_delta)).astype(jnp.bfloat16)
    grad_q = weigh_keys(grad_score, global_kv[0], window_kv[0], remote_kv[0]).astype(jnp.bfloat16)
    key_global, key_window, key_random = key_terms(grad_score, query_blocks)
    value_global, value_window, value_random = key_terms(weights, grad_blocks)
    global_sum = lax.psum(jnp.stack([key_global, value_global]).astype(jnp.bfloat16), "seq").astype(
        jnp.float32
    )
    window_grad = jnp.stack([key_window, value_window]).reshape(
        2, query_count, 3, BLK, head_count, HD
    )
    no_pad = (0, 0)
    extended = (
        jnp.pad(window_grad[:, :, 0], (no_pad, (0, 2), no_pad, no_pad, no_pad))
        + jnp.pad(window_grad[:, :, 1], (no_pad, (1, 1), no_pad, no_pad, no_pad))
        + jnp.pad(window_grad[:, :, 2], (no_pad, (2, 0), no_pad, no_pad, no_pad))
    )
    outward = jnp.concatenate([extended[:, 0], extended[:, query_count + 1]], axis=1)
    inward = with_halo(outward.astype(jnp.bfloat16), (("seq", 1),), BLK).astype(outward.dtype)
    own_grad = extended[:, 1 : query_count + 1]
    own_grad = own_grad.at[:, 0].add(inward[:, :BLK])
    own_grad = own_grad.at[:, query_count - 1].add(inward[:, 3 * BLK :])
    random_terms = (
        jnp.stack([key_random, value_random])
        .reshape(2, query_count * RAND, BLK, head_count, HD)
        .astype(jnp.bfloat16)
    )
    send_pick = (places[None, :] == jnp.arange(groups * capacity, dtype=jnp.int32)[:, None]).astype(
        jnp.bfloat16
    )
    outgoing = jnp.einsum(
        "pj,xjihd->xpihd", send_pick, random_terms, preferred_element_type=jnp.float32
    ).astype(jnp.bfloat16)
    incoming = lax.all_to_all(
        outgoing.reshape(2, groups, capacity, BLK, head_count, HD),
        "seq",
        split_axis=1,
        concat_axis=1,
        tiled=True,
    )
    take_pick = (
        wanted.reshape(-1)[None, :] == jnp.arange(query_count, dtype=jnp.int32)[:, None]
    ).astype(jnp.bfloat16)
    random_sum = jnp.einsum(
        "qp,xpihd->xqihd",
        take_pick,
        incoming.reshape(2, groups * capacity, BLK, head_count, HD),
        preferred_element_type=jnp.float32,
    )
    global_sum = global_sum.reshape(2, 2, BLK, head_count, HD)
    own_grad = own_grad.at[:, 0:2].add(jnp.where(my_group == 0, global_sum, 0.0))
    total_grad = own_grad + random_sum
    grad_k = total_grad[0].reshape(group_tokens, head_count * HD).astype(jnp.bfloat16)
    grad_v = total_grad[1].reshape(group_tokens, head_count * HD).astype(jnp.bfloat16)
    return (
        lax.all_to_all(
            attended.reshape(group_tokens, head_count * HD),
            "head",
            split_axis=0,
            concat_axis=1,
            tiled=True,
        ),
        lax.all_to_all(
            grad_q.reshape(group_tokens, head_count * HD),
            "head",
            split_axis=0,
            concat_axis=1,
            tiled=True,
        ),
        lax.all_to_all(grad_k, "head", split_axis=0, concat_axis=1, tiled=True),
        lax.all_to_all(grad_v, "head", split_axis=0, concat_axis=1, tiled=True),
    )


def solution(mesh):
    placed = (
        P(("seq", "head"), None),
        P(("seq", "head"), None),
        P(("seq", "head"), None),
        P(("seq", "head"), None),
        P("seq", None),
    )
    return jax.shard_map(
        shards,
        mesh=mesh,
        in_specs=placed,
        out_specs=(
            P(("seq", "head"), None),
            P(("seq", "head"), None),
            P(("seq", "head"), None),
            P(("seq", "head"), None),
        ),
        check_vma=False,
    )
```

profile of v0, /device:TPU:1, one launch (start us, length us, event | category | flops | bytes accessed | tf_op | source)
XLA Modules:
  0.0 558.6 jit_solution(16468300619809350168)
XLA Ops:
  7.2 0.8 copy.165
  9.3 13.7 %all-to-all-start.3 = ((s32[32,1,2]{2,1,0:T(1,128)}), s32[32,1,2]{2,1,0:T(1,128)S(1)}, u32[]{:S(2)}, u32[]{:S(2)}) async-start(s32[32,1,2]{2,1,0:T(1,128)} %bitcast.20), calls=%async_computation.3 | async-start | bytes 32768 | tf_op jit(solution)/shard_map/all_to_all | solution.py:125
  23.0 0.8 copy_bitcast_fusion.8
  23.8 7.7 %all-to-all-done.3 = s32[32,1,2]{2,1,0:T(1,128)S(1)} async-done(((s32[32,1,2]{2,1,0:T(1,128)}), s32[32,1,2]{2,1,0:T(1,128)S(1)}, u32[]{:S(2)}, u32[]{:S(2)}) %all-to-all-start.3) | async-done | bytes 288 | tf_op jit(solution)/shard_map/all_to_all | solution.py:125
  31.5 9.2 %all-to-all-start.2 = ((bf16[64,16,128]{2,0,1:T(8,128)(2,1)}), bf16[64,16,128]{2,0,1:T(8,128)(2,1)S(1)}, u32[]{:S(2)}, u32[]{:S(2)}) async-start(bf16[64,16,128]{2,0,1:T(8,128)(2,1)} %copy_bitcast_fusion.8), calls=%async_computation.2 | async-start | bytes 524288 | tf_op jit(solution)/shard_map/all_to_all | solution.py:104
  40.7 1.7 copy_bitcast_fusion.10
  42.4 10.0 %all-to-all-done.2 = bf16[64,16,128]{2,0,1:T(8,128)(2,1)S(1)} async-done(((bf16[64,16,128]{2,0,1:T(8,128)(2,1)}), bf16[64,16,128]{2,0,1:T(8,128)(2,1)S(1)}, u32[]{:S(2)}, u32[]{:S(2)}) %all-to-all-start.2) | async-done | bytes 262176 | tf_op jit(solution)/shard_map/all_to_all | solution.py:104
  52.4 3.4 all-to-all-start
  55.9 0.8 copy_bitcast_fusion.9
  56.6 0.8 copy_bitcast_fusion.7
  58.8 8.2 %all-to-all-done = bf16[64,16,128]{2,0,1:T(8,128)(2,1)S(1)} async-done(((bf16[64,16,128]{2,0,1:T(8,128)(2,1)}), bf16[64,16,128]{2,0,1:T(8,128)(2,1)S(1)}, u32[]{:S(2)}, u32[]{:S(2)}) %all-to-all-start) | async-done | bytes 262176 | tf_op jit(solution)/shard_map/all_to_all | solution.py:105
  67.0 3.4 all-to-all-start.1
  70.6 11.6 %all-to-all-done.1 = bf16[64,16,128]{2,0,1:T(8,128)(2,1)S(1)} async-done(((bf16[64,16,128]{2,0,1:T(8,128)(2,1)}), bf16[64,16,128]{2,0,1:T(8,128)(2,1)S(1)}, u32[]{:S(2)}, u32[]{:S(2)}) %all-to-all-start.1) | async-done | bytes 262176 | tf_op jit(solution)/shard_map/all_to_all | solution.py:106
  82.1 3.4 all-to-all-start.6
  85.6 3.0 gather_fusion
  88.7 2.7 copy.169
  91.9 2.5 copy.170
  94.4 2.3 all-to-all-done.6
  96.7 4.9 all-to-all-start.4
  101.9 3.0 collective-permute-start
  104.9 1.5 collective-permute-start.1
  107.0 7.4 %collective-permute-done = bf16[2,128,128]{2,1,0:T(8,128)(2,1)S(1)} collective-permute-done((bf16[2,128,128]{2,1,0:T(8,128)(2,1)S(1)}, bf16[2,128,128]{2,1,0:T(8,128)(2,1)S(1)}, u32[]{:S(2)}, u32[]{:S(2)}) %collective-permute-start) | collective-permute-done | bytes 65568 | tf_op jit(solution)/shard_map/ppermute | solution.py:19
  115.4 0.8 copy-done.6
  116.2 1.5 convolution_bitcast_fusion.1
  117.7 159.4 %all-reduce.6.cloned.1.call-done = bf16[2,256,1,128]{3,1,2,0:T(8,128)(2,1)} async-done(((bf16[2,256,1,128]{3,1,2,0:T(8,128)(2,1)}), bf16[2,256,1,128]{3,1,2,0:T(8,128)(2,1)}) %all-reduce.6.cloned.1.call-update) | async-done | bytes 131088 | tf_op jit(solution)/shard_map/psum | solution.py:30
  277.1 1.1 convolution_bitcast_fusion.6
  278.2 2.1 convolution_bitcast_fusion.5
  280.4 4.8 copy.171
  285.2 4.1 gather_fusion.1
  289.3 1.6 bitcast_select_fusion
  291.5 1.4 fusion.20
  292.9 1.5 fusion.2
  294.8 1.0 copy-done.8
  296.1 1.9 multiply_reduce_fusion
  298.0 2.3 multiply_convert_fusion
  302.9 1.4 convolution_convert_fusion
  304.3 6.7 %copy.190 = bf16[2,32,2,128,1,128]{5,2,3,0,4,1:T(2,128)(2,1)} copy(bf16[2,32,2,128,1,128]{5,2,1,3,0,4:T(2,128)(2,1)S(1)} %bitcast.319) | data formatting | bytes 8388608 | tf_op jit(solution)/shard_map/reshape | solution.py:182
  311.0 6.0 %all-to-all-start.8 = ((bf16[2,32,2,128,1,128]{5,2,3,0,4,1:T(2,128)(2,1)}), bf16[2,32,2,128,1,128]{5,2,3,0,4,1:T(2,128)(2,1)}, u32[]{:S(2)}, u32[]{:S(2)}) async-start(bf16[2,32,2,128,1,128]{5,2,3,0,4,1:T(2,128)(2,1)} %copy.190), calls=%async_computation.8 | async-start | bytes 8388608 | tf_op jit(solution)/shard_map/all_to_all | solution.py:181
  317.4 1.3 fusion.17
  319.7 1.5 fusion.22
  322.4 3.3 collective-permute-start.2
  325.8 1.4 collective-permute-start.3
  329.4 1.1 fusion.12
  330.5 1.1 fusion.13
  331.7 4.2 collective-permute-done.3
  336.7 3.0 scatter-add.11
  339.7 68.0 %all-to-all-done.8 = bf16[2,32,2,128,1,128]{5,2,3,0,4,1:T(2,128)(2,1)} async-done(((bf16[2,32,2,128,1,128]{5,2,3,0,4,1:T(2,128)(2,1)}), bf16[2,32,2,128,1,128]{5,2,3,0,4,1:T(2,128)(2,1)}, u32[]{:S(2)}, u32[]{:S(2)}) %all-to-all-start.8) | async-done | bytes 4194336 | tf_op jit(solution)/shard_map/all_to_all | solution.py:181
  407.7 14.6 %all-to-all-start.7 = ((bf16[16,64,128]{2,1,0:T(8,128)(2,1)}), bf16[16,64,128]{2,1,0:T(8,128)(2,1)S(1)}, u32[]{:S(2)}, u32[]{:S(2)}) async-start(bf16[16,64,128]{2,1,0:T(8,128)(2,1)} %bitcast.67), calls=%async_computation.7 | async-start | bytes 524288 | tf_op jit(solution)/shard_map/all_to_all | solution.py:210
  422.3 65.6 %all-reduce.8.cloned.1.call-done = bf16[2,256,1,128]{3,1,2,0:T(8,128)(2,1)} async-done(((bf16[2,256,1,128]{3,1,2,0:T(8,128)(2,1)}), bf16[2,256,1,128]{3,1,2,0:T(8,128)(2,1)}) %all-reduce.8.cloned.1.call-update) | async-done | bytes 131088 | tf_op jit(solution)/shard_map/psum | solution.py:153
  487.9 0.9 convert_select_fusion
  489.1 9.0 %copy.191 = bf16[2,32,2,128,1,128]{5,2,1,3,0,4:T(2,128)(2,1)} copy(bf16[2,32,2,128,1,128]{5,2,3,0,4,1:T(2,128)(2,1)} %all-to-all-done.8) | data formatting | bytes 8388608 | tf_op jit(solution)/shard_map/all_to_all | solution.py:181
  498.1 11.5 %all-to-all-start.5 = ((bf16[16,64,128]{2,1,0:T(8,128)(2,1)}), bf16[16,64,128]{2,1,0:T(8,128)(2,1)S(1)}, u32[]{:S(2)}, u32[]{:S(2)}) async-start(bf16[16,64,128]{2,1,0:T(8,128)(2,1)} %bitcast.45), calls=%async_computation.5 | async-start | bytes 524288 | tf_op jit(solution)/shard_map/all_to_all | solution.py:203
  509.7 2.8 fusion.7
  512.5 0.7 copy.194
  513.3 8.1 %all-to-all-done.5 = bf16[16,64,128]{2,1,0:T(8,128)(2,1)S(1)} async-done(((bf16[16,64,128]{2,1,0:T(8,128)(2,1)}), bf16[16,64,128]{2,1,0:T(8,128)(2,1)S(1)}, u32[]{:S(2)}, u32[]{:S(2)}) %all-to-all-start.5) | async-done | bytes 262176 | tf_op jit(solution)/shard_map/all_to_all | solution.py:203
  521.4 3.4 all-to-all-start.10
  524.8 0.7 copy_bitcast_fusion.5
  525.5 0.7 copy.192
  526.3 9.6 %all-to-all-done.10 = bf16[16,64,128]{2,1,0:T(8,128)(2,1)S(1)} async-done(((bf16[16,64,128]{2,1,0:T(8,128)(2,1)}), bf16[16,64,128]{2,1,0:T(8,128)(2,1)S(1)}, u32[]{:S(2)}, u32[]{:S(2)}) %all-to-all-start.10) | async-done | bytes 262176 | tf_op jit(solution)/shard_map/all_to_all | solution.py:218
  535.9 3.4 all-to-all-start.9
  539.4 0.7 copy_bitcast_fusion.6
  540.1 0.7 copy_bitcast_fusion.3
  540.8 10.2 %all-to-all-done.9 = bf16[16,64,128]{2,1,0:T(8,128)(2,1)S(1)} async-done(((bf16[16,64,128]{2,1,0:T(8,128)(2,1)}), bf16[16,64,128]{2,1,0:T(8,128)(2,1)S(1)}, u32[]{:S(2)}, u32[]{:S(2)}) %all-to-all-start.9) | async-done | bytes 262176 | tf_op jit(solution)/shard_map/all_to_all | solution.py:217
  551.1 0.7 copy_bitcast_fusion.4
  (108 shorter events, 14.6 us)
Async XLA Ops:
  7.2 15.8 %copy-start = (bf16[64,2048]{1,0:T(8,128)(2,1)S(1)}, bf16[64,2048]{1,0:T(8,128)(2,1)}, u32[]{:S(2)}) copy-start(bf16[64,2048]{1,0:T(8,128)(2,1)} %param.11) | copy-start | bytes 786436
  7.2 48.7 %copy-start.17 = (bf16[64,2048]{1,0:T(8,128)(2,1)S(1)}, bf16[64,2048]{1,0:T(8,128)(2,1)}, u32[]{:S(2)}) copy-start(bf16[64,2048]{1,0:T(8,128)(2,1)} %param.13) | copy-start | bytes 786436
  7.2 49.4 %copy-start.18 = (bf16[64,2048]{1,0:T(8,128)(2,1)S(1)}, bf16[64,2048]{1,0:T(8,128)(2,1)}, u32[]{:S(2)}) copy-start(bf16[64,2048]{1,0:T(8,128)(2,1)} %param.14) | copy-start | bytes 786436
  9.3 22.2 %all-to-all-start.3 = ((s32[32,1,2]{2,1,0:T(1,128)}), s32[32,1,2]{2,1,0:T(1,128)S(1)}, u32[]{:S(2)}, u32[]{:S(2)}) async-start(s32[32,1,2]{2,1,0:T(1,128)} %bitcast.20), calls=%async_computation.3 | async-start | bytes 32768 | tf_op jit(solution)/shard_map/all_to_all | solution.py:125
  31.5 20.9 %all-to-all-start.2 = ((bf16[64,16,128]{2,0,1:T(8,128)(2,1)}), bf16[64,16,128]{2,0,1:T(8,128)(2,1)S(1)}, u32[]{:S(2)}, u32[]{:S(2)}) async-start(bf16[64,16,128]{2,0,1:T(8,128)(2,1)} %copy_bitcast_fusion.8), calls=%async_computation.2 | async-start | bytes 524288 | tf_op jit(solution)/shard_map/all_to_all | solution.py:104
  52.4 14.6 %all-to-all-start = ((bf16[64,16,128]{2,0,1:T(8,128)(2,1)}), bf16[64,16,128]{2,0,1:T(8,128)(2,1)S(1)}, u32[]{:S(2)}, u32[]{:S(2)}) async-start(bf16[64,16,128]{2,0,1:T(8,128)(2,1)} %copy_bitcast_fusion.10), calls=%async_computation | async-start | bytes 524288 | tf_op jit(solution)/shard_map/all_to_all | solution.py:105
  67.0 15.1 %all-to-all-start.1 = ((bf16[64,16,128]{2,0,1:T(8,128)(2,1)}), bf16[64,16,128]{2,0,1:T(8,128)(2,1)S(1)}, u32[]{:S(2)}, u32[]{:S(2)}) async-start(bf16[64,16,128]{2,0,1:T(8,128)(2,1)} %copy_bitcast_fusion.9), calls=%async_computation.1 | async-start | bytes 524288 | tf_op jit(solution)/shard_map/all_to_all | solution.py:106
  82.1 14.5 %all-to-all-start.6 = ((bf16[64,16,128]{2,0,1:T(8,128)(2,1)}), bf16[64,16,128]{2,0,1:T(8,128)(2,1)S(1)}, u32[]{:S(2)}, u32[]{:S(2)}) async-start(bf16[64,16,128]{2,0,1:T(8,128)(2,1)} %copy_bitcast_fusion.7), calls=%async_computation.6 | async-start | bytes 524288 | tf_op jit(solution)/shard_map/all_to_all | solution.py:107
  96.7 183.7 %all-to-all-start.4 = ((bf16[2,32,2,128,1,128]{5,3,2,0,4,1:T(8,128)(2,1)}), bf16[2,32,2,128,1,128]{5,3,2,0,4,1:T(8,128)(2,1)}, u32[]{:S(2)}, u32[]{:S(2)}) async-start(bf16[2,32,2,128,1,128]{5,3,2,0,4,1:T(8,128)(2,1)} %copy.170), calls=%async_computation.4 | async-start | bytes 8388608 | tf_op jit(solution)/shard_map/all_to_all | solution.py:134
  101.5 175.6 %all-reduce.6.cloned.1.call-start = ((), (), s32[]{:S(2)}) async-start(), calls=%async_computation.11 | async-start | bytes 262144 | tf_op jit(solution)/shard_map/psum | solution.py:30
  101.9 12.5 %collective-permute-start = (bf16[2,128,128]{2,1,0:T(8,128)(2,1)S(1)}, bf16[2,128,128]{2,1,0:T(8,128)(2,1)S(1)}, u32[]{:S(2)}, u32[]{:S(2)}) collective-permute-start(bf16[2,128,128]{2,1,0:T(8,128)(2,1)S(1)} %get-tuple-element.58), channel_id=1, source_target_pairs={{0,1},{1,2},{2,3},{3,4},{4,5},{5,6},{6,7},{7,8},{8,9},{9,10},{10,1... | collective-permute-start | bytes 196616 | tf_op jit(solution)/shard_map/ppermute | solution.py:19
  104.9 9.6 %collective-permute-start.1 = (bf16[2,128,128]{2,1,0:T(8,128)(2,1)S(1)}, bf16[2,128,128]{2,1,0:T(8,128)(2,1)S(1)}, u32[]{:S(2)}, u32[]{:S(2)}) collective-permute-start(bf16[2,128,128]{2,1,0:T(8,128)(2,1)S(1)} %get-tuple-element.59), channel_id=1, source_target_pairs={{1,0},{2,1},{3,2},{4,3},{5,4},{6,5},{7,6},{8,7},{9,8},{10,9},{11,1... | collective-permute-start | bytes 196616 | tf_op jit(solution)/shard_map/ppermute | solution.py:21
  115.0 1.1 copy-start.6
  291.1 1.8 copy-start.10
  291.1 3.3 copy-start.12
  294.4 1.4 copy-start.8
  294.4 1.7 copy-start.9
  300.4 1.4 copy-start.2
  300.4 2.0 copy-start.4
  311.0 7.8 %copy-start.3 = (bf16[8,1,128,1024]{2,3,0,1:T(8,128)(2,1)S(1)}, bf16[8,1,128,1024]{2,3,0,1:T(8,128)(2,1)}, u32[]{:S(2)}) copy-start(bf16[8,1,128,1024]{2,3,0,1:T(8,128)(2,1)} %copy-done.2) | copy-start | bytes 6291460
  311.0 96.8 %all-to-all-start.8 = ((bf16[2,32,2,128,1,128]{5,2,3,0,4,1:T(2,128)(2,1)}), bf16[2,32,2,128,1,128]{5,2,3,0,4,1:T(2,128)(2,1)}, u32[]{:S(2)}, u32[]{:S(2)}) async-start(bf16[2,32,2,128,1,128]{5,2,3,0,4,1:T(2,128)(2,1)} %copy.190), calls=%async_computation.8 | async-start | bytes 8388608 | tf_op jit(solution)/shard_map/all_to_all | solution.py:181
  317.0 170.9 %all-reduce.8.cloned.1.call-start = ((), (), s32[]{:S(2)}) async-start(), calls=%async_computation.12 | async-start | bytes 262144 | tf_op jit(solution)/shard_map/psum | solution.py:153
  322.1 5.1 copy-start.16
  322.4 5.6 copy-start.14
  322.4 4.9 copy-start.5
  322.4 5.6 copy-start.13
  322.4 9.2 %collective-permute-start.2 = (bf16[2,128,1,128]{3,1,0,2:T(8,128)(2,1)S(1)}, bf16[2,128,1,128]{3,1,0,2:T(8,128)(2,1)S(1)}, u32[]{:S(2)}, u32[]{:S(2)}) collective-permute-start(bf16[2,128,1,128]{3,1,0,2:T(8,128)(2,1)S(1)} %get-tuple-element.49), channel_id=1, source_target_pairs={{0,1},{1,2},{2,3},{3,4},{4,5},{5,6},{6,7},{7,8},{8,9},{9,10},{10,1... | collective-permute-start | bytes 196616 | tf_op jit(solution)/shard_map/ppermute | solution.py:19
  325.8 2.6 copy-start.11
  325.8 10.1 %collective-permute-start.3 = (bf16[2,128,1,128]{3,1,0,2:T(8,128)(2,1)S(1)}, bf16[2,128,1,128]{3,1,0,2:T(8,128)(2,1)S(1)}, u32[]{:S(2)}, u32[]{:S(2)}) collective-permute-start(bf16[2,128,1,128]{3,1,0,2:T(8,128)(2,1)S(1)} %get-tuple-element.50), channel_id=1, source_target_pairs={{1,0},{2,1},{3,2},{4,3},{5,4},{6,5},{7,6},{8,7},{9,8},{10,9},{11,1... | collective-permute-start | bytes 196616 | tf_op jit(solution)/shard_map/ppermute | solution.py:21
  327.9 1.4 copy-start.7
  330.5 5.4 copy-start.15
  330.5 5.4 slice-start
  407.7 90.4 %all-to-all-start.7 = ((bf16[16,64,128]{2,1,0:T(8,128)(2,1)}), bf16[16,64,128]{2,1,0:T(8,128)(2,1)S(1)}, u32[]{:S(2)}, u32[]{:S(2)}) async-start(bf16[16,64,128]{2,1,0:T(8,128)(2,1)} %bitcast.67), calls=%async_computation.7 | async-start | bytes 524288 | tf_op jit(solution)/shard_map/all_to_all | solution.py:210
  498.1 23.2 %all-to-all-start.5 = ((bf16[16,64,128]{2,1,0:T(8,128)(2,1)}), bf16[16,64,128]{2,1,0:T(8,128)(2,1)S(1)}, u32[]{:S(2)}, u32[]{:S(2)}) async-start(bf16[16,64,128]{2,1,0:T(8,128)(2,1)} %bitcast.45), calls=%async_computation.5 | async-start | bytes 524288 | tf_op jit(solution)/shard_map/all_to_all | solution.py:203
  512.5 39.3 %copy-start.1 = (bf16[64,2048]{1,0:T(8,128)(2,1)S(1)}, bf16[64,2048]{1,0:T(8,128)(2,1)}, u32[]{:S(2)}) copy-start(bf16[64,2048]{1,0:T(8,128)(2,1)} %param.11) | copy-start | bytes 786436
  521.4 14.6 %all-to-all-start.10 = ((bf16[16,64,128]{2,1,0:T(8,128)(2,1)}), bf16[16,64,128]{2,1,0:T(8,128)(2,1)S(1)}, u32[]{:S(2)}, u32[]{:S(2)}) async-start(bf16[16,64,128]{2,1,0:T(8,128)(2,1)} %bitcast.126), calls=%async_computation.10 | async-start | bytes 524288 | tf_op jit(solution)/shard_map/all_to_all | solution.py:218
  535.9 15.1 %all-to-all-start.9 = ((bf16[16,64,128]{2,1,0:T(8,128)(2,1)}), bf16[16,64,128]{2,1,0:T(8,128)(2,1)S(1)}, u32[]{:S(2)}, u32[]{:S(2)}) async-start(bf16[16,64,128]{2,1,0:T(8,128)(2,1)} %bitcast.124), calls=%async_computation.9 | async-start | bytes 524288 | tf_op jit(solution)/shard_map/all_to_all | solution.py:217
Sparse Core Ops, SparseCore 0:
  107.2 169.8 all-reduce.5
  322.3 165.5 all-reduce.7
where the time goes:
time: 560 us; the launch traced here: 559 us
  waiting for transfers between devices  372 us (66%)
  starting transfers between devices  86.6 us (15%)
  local copies, waits for them, and re-layouts  53 us (9%)
  matrix products  18.1 us (3%)
  between operations  14.7 us (3%)
  other arithmetic  13.9 us (2%)
    psum x1, waiting for transfers between devices, broadcast(): return lax.psum(kept, axis)  159 us
    all_to_all x1, waiting for transfers between devices, shards(): lax.all_to_all(outgoing.reshape(2, groups, capacity, BLK, head_count, HD)...  68 us
    psum x1, waiting for transfers between devices, shards(): lax.psum(jnp.stack([key_global, value_global]).astype(jnp.bfloat16), 'seq')  65.6 us
    all_to_all x1, starting transfers between devices, shards(): lax.all_to_all(grad_q.reshape(group_tokens, head_count * HD), 'head', spl...  14.6 us
    all_to_all x1, starting transfers between devices, shards(): lax.all_to_all(request_table(random_blocks, query_count, groups, capacity...  13.7 us
    all_to_all x1, waiting for transfers between devices, shards(): lax.all_to_all(values, 'head', split_axis=1, concat_axis=0, tiled=True)  11.6 us
    all_to_all x1, starting transfers between devices, shards(): lax.all_to_all(attended.reshape(group_tokens, head_count * HD), 'head', s...  11.5 us
  transfers between devices with their start and end apart: 17, of which 13 were waited for; matrix products, arithmetic and copies ran while one was open for 9% of the time, Pallas kernels for 0%

commit v1 on v0

--- a/solution.py
+++ b/solution.py
@@ -25,9 +25,28 @@
     return cells
 
 
-def broadcast(value, axis, source):
-    kept = jnp.where(lax.axis_index(axis) == source, value, 0).astype(value.dtype)
-    return lax.psum(kept, axis)
+def broadcast(value, axis):
+    count = lax.axis_size(axis)
+    me = lax.axis_index(axis)
+    step = 1
+    while step < count:
+        pairs = [(i, i + step) for i in range(step) if i + step < count]
+        got = lax.ppermute(value, axis, pairs)
+        value = jnp.where((me >= step) & (me < 2 * step), got, value)
+        step *= 2
+    return value
+
+
+def reduce_to_first(value, axis):
+    count = lax.axis_size(axis)
+    step = 1
+    while step * 2 < count:
+        step *= 2
+    while step >= 1:
+        pairs = [(i + step, i) for i in range(step) if i + step < count]
+        value = value + lax.ppermute(value, axis, pairs)
+        step //= 2
+    return value
 
 
 def slot_places(owners, groups, capacity):
@@ -119,7 +138,7 @@
         [edged[:, 0:query_count], edged[:, 1 : query_count + 1], edged[:, 2 : query_count + 2]],
         axis=2,
     )
-    global_kv = broadcast(kv_blocks[:, 0:2].reshape(2, 2 * BLK, head_count, HD), "seq", 0)
+    global_kv = broadcast(kv_blocks[:, 0:2].reshape(2, 2 * BLK, head_count, HD), "seq")
     flat_ids = random_blocks.reshape(-1)
     places = slot_places(flat_ids // query_count, groups, capacity)
     wanted = lax.all_to_all(
@@ -150,9 +169,7 @@
     grad_q = weigh_keys(grad_score, global_kv[0], window_kv[0], remote_kv[0]).astype(jnp.bfloat16)
     key_global, key_window, key_random = key_terms(grad_score, query_blocks)
     value_global, value_window, value_random = key_terms(weights, grad_blocks)
-    global_sum = lax.psum(jnp.stack([key_global, value_global]).astype(jnp.bfloat16), "seq").astype(
-        jnp.float32
-    )
+    global_sum = reduce_to_first(jnp.stack([key_global, value_global]), "seq")
     window_grad = jnp.stack([key_window, value_window]).reshape(
         2, query_count, 3, BLK, head_count, HD
     )

time: 560 us -> 461 us (0.82)
  waiting for transfers between devices: 372 us -> 195 us
  starting transfers between devices: 86.6 us -> 182 us
  between operations: 14.7 us -> 1.49 us
    psum x2 -> x0, waiting for transfers between devices: 225 us -> none  [the longest x1 159 us: broadcast(): return lax.psum(kept, axis)]
    ppermute x0 -> x10, waiting for transfers between devices: none -> 121 us  [the longest x5 112 us: reduce_to_first(): value = value + lax.ppermute(value, axis, pairs)]
    ppermute x0 -> x10, starting transfers between devices: none -> 94.8 us  [the longest x5 88.2 us: broadcast(): got = lax.ppermute(value, axis, pairs)]
    all_to_all x1, waiting for transfers between devices: 68 us -> 0.01 us  [shards(): lax.all_to_all(outgoing.reshape(2, groups, capacity, BLK, head_count, HD)...]
    all_to_all x1, starting transfers between devices: 6.05 us -> 17.8 us  [shards(): lax.all_to_all(outgoing.reshape(2, groups, capacity, BLK, head_count, HD)...]
    all_to_all x1, starting transfers between devices: 14.6 us -> 4.77 us  [shards(): lax.all_to_all(grad_q.reshape(group_tokens, head_count * HD), 'head', spl...]
    all_to_all x1, waiting for transfers between devices: 0.01 us -> 8.06 us  [shards(): lax.all_to_all(grad_q.reshape(group_tokens, head_count * HD), 'head', spl...]
  transfers between devices with their start and end apart: 17 -> 25, of which waited for: 13 -> 19; matrix products, arithmetic and copies ran while one was open for 9% -> 10% of each run, Pallas kernels for 0% -> 0%
where the time goes in v1:
time: 461 us; the launch traced here: 459 us
  waiting for transfers between devices  195 us (42%)
  starting transfers between devices  182 us (39%)
  local copies, waits for them, and re-layouts  52.9 us (11%)
  matrix products  15.5 us (3%)
  other arithmetic  11.9 us (3%)
    ppermute x5, waiting for transfers between devices, reduce_to_first(): value = value + lax.ppermute(value, axis, pairs)  112 us
    ppermute x5, starting transfers between devices, broadcast(): got = lax.ppermute(value, axis, pairs)  88.2 us
    all_to_all x1, starting transfers between devices, shards(): lax.all_to_all(outgoing.reshape(2, groups, capacity, BLK, head_count, HD)...  17.8 us
    all_to_all x1, starting transfers between devices, shards(): lax.all_to_all(request_table(random_blocks, query_count, groups, capacity...  13.7 us
    all_to_all x1, waiting for transfers between devices, shards(): lax.all_to_all(values, 'head', split_axis=1, concat_axis=0, tiled=True)  11.6 us
    all_to_all x1, starting transfers between devices, shards(): lax.all_to_all(attended.reshape(group_tokens, head_count * HD), 'head', s...  10.2 us
    all_to_all x1, waiting for transfers between devices, shards(): lax.all_to_all(grad_k, 'head', split_axis=0, concat_axis=1, tiled=True)  10.2 us
    all_to_all x1, waiting for transfers between devices, shards(): lax.all_to_all(queries, 'head', split_axis=1, concat_axis=0, tiled=True)  9.99 us
  transfers between devices with their start and end apart: 25, of which 19 were waited for; matrix products, arithmetic and copies ran while one was open for 10% of the time, Pallas kernels for 0%

profile of v1, /device:TPU:1, one launch (start us, length us, event | category | flops | bytes accessed | tf_op | source)
XLA Modules:
  0.0 459.5 jit_solution(10940676813869439960)
XLA Ops:
  2.7 13.7 %all-to-all-start.3 = ((s32[32,1,2]{2,1,0:T(1,128)}), s32[32,1,2]{2,1,0:T(1,128)S(1)}, u32[]{:S(2)}, u32[]{:S(2)}) async-start(s32[32,1,2]{2,1,0:T(1,128)} %bitcast.20), calls=%async_computation.3 | async-start | bytes 32768 | tf_op jit(solution)/shard_map/all_to_all | solution.py:144
  17.2 7.7 %all-to-all-done.3 = s32[32,1,2]{2,1,0:T(1,128)S(1)} async-done(((s32[32,1,2]{2,1,0:T(1,128)}), s32[32,1,2]{2,1,0:T(1,128)S(1)}, u32[]{:S(2)}, u32[]{:S(2)}) %all-to-all-start.3) | async-done | bytes 288 | tf_op jit(solution)/shard_map/all_to_all | solution.py:144
  25.0 9.2 %all-to-all-start.2 = ((bf16[64,16,128]{2,0,1:T(8,128)(2,1)}), bf16[64,16,128]{2,0,1:T(8,128)(2,1)S(1)}, u32[]{:S(2)}, u32[]{:S(2)}) async-start(bf16[64,16,128]{2,0,1:T(8,128)(2,1)} %copy_bitcast_fusion.8), calls=%async_computation.2 | async-start | bytes 524288 | tf_op jit(solution)/shard_map/all_to_all | solution.py:123
  34.2 1.7 copy_bitcast_fusion.10
  35.9 10.0 %all-to-all-done.2 = bf16[64,16,128]{2,0,1:T(8,128)(2,1)S(1)} async-done(((bf16[64,16,128]{2,0,1:T(8,128)(2,1)}), bf16[64,16,128]{2,0,1:T(8,128)(2,1)S(1)}, u32[]{:S(2)}, u32[]{:S(2)}) %all-to-all-start.2) | async-done | bytes 262176 | tf_op jit(solution)/shard_map/all_to_all | solution.py:123
  45.9 3.4 all-to-all-start
  52.3 8.2 %all-to-all-done = bf16[64,16,128]{2,0,1:T(8,128)(2,1)S(1)} async-done(((bf16[64,16,128]{2,0,1:T(8,128)(2,1)}), bf16[64,16,128]{2,0,1:T(8,128)(2,1)S(1)}, u32[]{:S(2)}, u32[]{:S(2)}) %all-to-all-start) | async-done | bytes 262176 | tf_op jit(solution)/shard_map/all_to_all | solution.py:124
  60.4 3.4 all-to-all-start.1
  64.0 11.6 %all-to-all-done.1 = bf16[64,16,128]{2,0,1:T(8,128)(2,1)S(1)} async-done(((bf16[64,16,128]{2,0,1:T(8,128)(2,1)}), bf16[64,16,128]{2,0,1:T(8,128)(2,1)S(1)}, u32[]{:S(2)}, u32[]{:S(2)}) %all-to-all-start.1) | async-done | bytes 262176 | tf_op jit(solution)/shard_map/all_to_all | solution.py:125
  75.6 3.4 all-to-all-start.6
  79.1 3.1 gather_fusion
  82.1 2.7 copy.169
  85.3 2.5 copy.170
  87.9 2.3 all-to-all-done.6
  90.1 4.9 %all-to-all-start.4 = ((bf16[2,32,2,128,1,128]{5,3,2,0,4,1:T(8,128)(2,1)}), bf16[2,32,2,128,1,128]{5,3,2,0,4,1:T(8,128)(2,1)}, u32[]{:S(2)}, u32[]{:S(2)}) async-start(bf16[2,32,2,128,1,128]{5,3,2,0,4,1:T(8,128)(2,1)} %copy.170), calls=%async_computation.4 | async-start | bytes 8388608 | tf_op jit(solution)/shard_map/all_to_all | solution.py:153
  95.3 3.0 collective-permute-start.5
  98.3 1.3 collective-permute-start.6
  99.6 4.0 collective-permute-start
  103.6 4.3 collective-permute-done.5
  108.0 3.8 collective-permute-done
  111.8 3.0 collective-permute-start.1
  115.1 1.6 collective-permute-done.1
  116.7 78.4 %collective-permute-start.2 = (bf16[2,256,1,128]{3,1,2,0:T(8,128)(2,1)S(1)}, bf16[2,256,1,128]{3,1,2,0:T(8,128)(2,1)S(1)}, u32[]{:S(2)}, u32[]{:S(2)}) collective-permute-start(bf16[2,256,1,128]{3,1,2,0:T(8,128)(2,1)S(1)} %broadcast_select_fusion.2), channel_id=1, source_target_pairs={{0,4},{1,5},{2,6},{3,7},{32,36},{33,37},{34,38},{35,39},{64,68},{6... | collective-permute-start | bytes 393224 | tf_op jit(solution)/shard_map/ppermute | solution.py:34
  195.3 1.8 collective-permute-done.2
  197.1 1.3 collective-permute-start.3
  198.8 1.5 collective-permute-done.3
  200.3 1.5 collective-permute-start.4
  201.8 1.5 convolution_bitcast_fusion.1
  204.0 1.3 convolution_bitcast_fusion.5
  205.3 4.8 %copy.171 = bf16[2,32,2,128,1,128]{5,3,2,1,0,4:T(8,128)(2,1)} copy(bf16[2,32,2,128,1,128]{5,3,2,0,4,1:T(8,128)(2,1)} %all-to-all-done.4) | data formatting | bytes 8388608 | tf_op jit(solution)/shard_map/all_to_all | solution.py:153
  210.1 4.1 gather_fusion.1
  214.3 1.6 bitcast_select_fusion
  216.5 1.4 fusion.16
  217.9 1.5 fusion.2
  221.1 1.9 multiply_reduce_fusion
  223.0 2.3 multiply_convert_fusion
  227.9 1.4 convolution_convert_fusion
  229.2 6.7 %copy.190 = bf16[2,32,2,128,1,128]{5,2,3,0,4,1:T(2,128)(2,1)} copy(bf16[2,32,2,128,1,128]{5,2,1,3,0,4:T(2,128)(2,1)S(1)} %bitcast.311) | data formatting | bytes 8388608 | tf_op jit(solution)/shard_map/reshape | solution.py:199
  235.9 17.8 %all-to-all-start.8 = ((bf16[2,32,2,128,1,128]{5,2,3,0,4,1:T(2,128)(2,1)}), bf16[2,32,2,128,1,128]{5,2,3,0,4,1:T(2,128)(2,1)}, u32[]{:S(2)}, u32[]{:S(2)}) async-start(bf16[2,32,2,128,1,128]{5,2,3,0,4,1:T(2,128)(2,1)} %copy.190), calls=%async_computation.8 | async-start | bytes 8388608 | tf_op jit(solution)/shard_map/all_to_all | solution.py:198
  254.1 1.5 convolution_bitcast_fusion.13
  255.6 1.5 collective-permute-start.9
  260.8 92.3 %collective-permute-done.9 = f32[2,256,1,128]{3,1,2,0:T(8,128)S(1)} collective-permute-done((f32[2,256,1,128]{3,1,2,0:T(8,128)S(1)}, f32[2,256,1,128]{3,1,2,0:T(8,128)S(1)}, u32[]{:S(2)}, u32[]{:S(2)}) %collective-permute-start.9) | collective-permute-done | bytes 262176 | tf_op jit(solution)/shard_map/ppermute | solution.py:47
  353.2 1.3 collective-permute-start.10
  354.9 4.1 collective-permute-start.7
  359.0 1.3 collective-permute-start.8
  360.8 6.2 %collective-permute-done.10 = f32[2,256,1,128]{3,1,2,0:T(8,128)S(1)} collective-permute-done((f32[2,256,1,128]{3,1,2,0:T(8,128)S(1)}, f32[2,256,1,128]{3,1,2,0:T(8,128)S(1)}, u32[]{:S(2)}, u32[]{:S(2)}) %collective-permute-start.10) | collective-permute-done | bytes 262176 | tf_op jit(solution)/shard_map/ppermute | solution.py:47
  367.0 1.3 collective-permute-start.11
  368.3 1.1 fusion.13
  369.4 7.3 %collective-permute-done.11 = f32[2,256,1,128]{3,1,2,0:T(8,128)S(1)} collective-permute-done((f32[2,256,1,128]{3,1,2,0:T(8,128)S(1)}, f32[2,256,1,128]{3,1,2,0:T(8,128)S(1)}, u32[]{:S(2)}, u32[]{:S(2)}) %collective-permute-start.11) | collective-permute-done | bytes 262176 | tf_op jit(solution)/shard_map/ppermute | solution.py:47
  376.7 1.3 collective-permute-start.12
  378.0 1.1 fusion.12
  379.0 6.3 %collective-permute-done.12 = f32[2,256,1,128]{3,1,2,0:T(8,128)S(1)} collective-permute-done((f32[2,256,1,128]{3,1,2,0:T(8,128)S(1)}, f32[2,256,1,128]{3,1,2,0:T(8,128)S(1)}, u32[]{:S(2)}, u32[]{:S(2)}) %collective-permute-start.12) | collective-permute-done | bytes 262176 | tf_op jit(solution)/shard_map/ppermute | solution.py:47
  385.3 1.3 collective-permute-start.13
  387.5 3.0 scatter-add.11
  390.5 10.2 %all-to-all-start.5 = ((bf16[16,64,128]{2,1,0:T(8,128)(2,1)}), bf16[16,64,128]{2,1,0:T(8,128)(2,1)S(1)}, u32[]{:S(2)}, u32[]{:S(2)}) async-start(bf16[16,64,128]{2,1,0:T(8,128)(2,1)} %bitcast.45), calls=%async_computation.5 | async-start | bytes 524288 | tf_op jit(solution)/shard_map/all_to_all | solution.py:220
  401.0 9.0 %copy.191 = bf16[2,32,2,128,1,128]{5,2,1,3,0,4:T(2,128)(2,1)} copy(bf16[2,32,2,128,1,128]{5,2,3,0,4,1:T(2,128)(2,1)} %all-to-all-done.8) | data formatting | bytes 8388608 | tf_op jit(solution)/shard_map/all_to_all | solution.py:198
  410.0 2.5 all-to-all-done.5
  412.6 4.8 %all-to-all-start.7 = ((bf16[16,64,128]{2,1,0:T(8,128)(2,1)}), bf16[16,64,128]{2,1,0:T(8,128)(2,1)S(1)}, u32[]{:S(2)}, u32[]{:S(2)}) async-start(bf16[16,64,128]{2,1,0:T(8,128)(2,1)} %bitcast.67), calls=%async_computation.7 | async-start | bytes 524288 | tf_op jit(solution)/shard_map/all_to_all | solution.py:227
  417.3 2.8 fusion.7
  421.0 8.1 %all-to-all-done.7 = bf16[16,64,128]{2,1,0:T(8,128)(2,1)S(1)} async-done(((bf16[16,64,128]{2,1,0:T(8,128)(2,1)}), bf16[16,64,128]{2,1,0:T(8,128)(2,1)S(1)}, u32[]{:S(2)}, u32[]{:S(2)}) %all-to-all-start.7) | async-done | bytes 262176 | tf_op jit(solution)/shard_map/all_to_all | solution.py:227
  429.0 3.4 all-to-all-start.10
  433.9 9.6 %all-to-all-done.10 = bf16[16,64,128]{2,1,0:T(8,128)(2,1)S(1)} async-done(((bf16[16,64,128]{2,1,0:T(8,128)(2,1)}), bf16[16,64,128]{2,1,0:T(8,128)(2,1)S(1)}, u32[]{:S(2)}, u32[]{:S(2)}) %all-to-all-start.10) | async-done | bytes 262176 | tf_op jit(solution)/shard_map/all_to_all | solution.py:235
  443.6 3.4 all-to-all-start.9
  448.5 10.2 %all-to-all-done.9 = bf16[16,64,128]{2,1,0:T(8,128)(2,1)S(1)} async-done(((bf16[16,64,128]{2,1,0:T(8,128)(2,1)}), bf16[16,64,128]{2,1,0:T(8,128)(2,1)S(1)}, u32[]{:S(2)}, u32[]{:S(2)}) %all-to-all-start.9) | async-done | bytes 262176 | tf_op jit(solution)/shard_map/all_to_all | solution.py:234
  (129 shorter events, 23.6 us)
Async XLA Ops:
  0.6 15.8 %copy-start = (bf16[64,2048]{1,0:T(8,128)(2,1)S(1)}, bf16[64,2048]{1,0:T(8,128)(2,1)}, u32[]{:S(2)}) copy-start(bf16[64,2048]{1,0:T(8,128)(2,1)} %param.11) | copy-start | bytes 786436
  0.6 48.7 %copy-start.16 = (bf16[64,2048]{1,0:T(8,128)(2,1)S(1)}, bf16[64,2048]{1,0:T(8,128)(2,1)}, u32[]{:S(2)}) copy-start(bf16[64,2048]{1,0:T(8,128)(2,1)} %param.13) | copy-start | bytes 786436
  0.7 49.4 %copy-start.17 = (bf16[64,2048]{1,0:T(8,128)(2,1)S(1)}, bf16[64,2048]{1,0:T(8,128)(2,1)}, u32[]{:S(2)}) copy-start(bf16[64,2048]{1,0:T(8,128)(2,1)} %param.14) | copy-start | bytes 786436
  2.7 22.2 %all-to-all-start.3 = ((s32[32,1,2]{2,1,0:T(1,128)}), s32[32,1,2]{2,1,0:T(1,128)S(1)}, u32[]{:S(2)}, u32[]{:S(2)}) async-start(s32[32,1,2]{2,1,0:T(1,128)} %bitcast.20), calls=%async_computation.3 | async-start | bytes 32768 | tf_op jit(solution)/shard_map/all_to_all | solution.py:144
  25.0 20.9 %all-to-all-start.2 = ((bf16[64,16,128]{2,0,1:T(8,128)(2,1)}), bf16[64,16,128]{2,0,1:T(8,128)(2,1)S(1)}, u32[]{:S(2)}, u32[]{:S(2)}) async-start(bf16[64,16,128]{2,0,1:T(8,128)(2,1)} %copy_bitcast_fusion.8), calls=%async_computation.2 | async-start | bytes 524288 | tf_op jit(solution)/shard_map/all_to_all | solution.py:123
  45.9 14.6 %all-to-all-start = ((bf16[64,16,128]{2,0,1:T(8,128)(2,1)}), bf16[64,16,128]{2,0,1:T(8,128)(2,1)S(1)}, u32[]{:S(2)}, u32[]{:S(2)}) async-start(bf16[64,16,128]{2,0,1:T(8,128)(2,1)} %copy_bitcast_fusion.10), calls=%async_computation | async-start | bytes 524288 | tf_op jit(solution)/shard_map/all_to_all | solution.py:124
  60.4 15.1 %all-to-all-start.1 = ((bf16[64,16,128]{2,0,1:T(8,128)(2,1)}), bf16[64,16,128]{2,0,1:T(8,128)(2,1)S(1)}, u32[]{:S(2)}, u32[]{:S(2)}) async-start(bf16[64,16,128]{2,0,1:T(8,128)(2,1)} %copy_bitcast_fusion.9), calls=%async_computation.1 | async-start | bytes 524288 | tf_op jit(solution)/shard_map/all_to_all | solution.py:125
  75.6 14.5 %all-to-all-start.6 = ((bf16[64,16,128]{2,0,1:T(8,128)(2,1)}), bf16[64,16,128]{2,0,1:T(8,128)(2,1)S(1)}, u32[]{:S(2)}, u32[]{:S(2)}) async-start(bf16[64,16,128]{2,0,1:T(8,128)(2,1)} %copy_bitcast_fusion.7), calls=%async_computation.6 | async-start | bytes 524288 | tf_op jit(solution)/shard_map/all_to_all | solution.py:126
  90.1 115.2 %all-to-all-start.4 = ((bf16[2,32,2,128,1,128]{5,3,2,0,4,1:T(8,128)(2,1)}), bf16[2,32,2,128,1,128]{5,3,2,0,4,1:T(8,128)(2,1)}, u32[]{:S(2)}, u32[]{:S(2)}) async-start(bf16[2,32,2,128,1,128]{5,3,2,0,4,1:T(8,128)(2,1)} %copy.170), calls=%async_computation.4 | async-start | bytes 8388608 | tf_op jit(solution)/shard_map/all_to_all | solution.py:153
  95.3 12.6 %collective-permute-start.5 = (bf16[2,128,128]{2,1,0:T(8,128)(2,1)S(1)}, bf16[2,128,128]{2,1,0:T(8,128)(2,1)S(1)}, u32[]{:S(2)}, u32[]{:S(2)}) collective-permute-start(bf16[2,128,128]{2,1,0:T(8,128)(2,1)S(1)} %get-tuple-element.58), channel_id=1, source_target_pairs={{0,1},{1,2},{2,3},{3,4},{4,5},{5,6},{6,7},{7,8},{8,9},{9,10},{10,1... | collective-permute-start | bytes 196616 | tf_op jit(solution)/shard_map/ppermute | solution.py:19
  98.3 9.6 %collective-permute-start.6 = (bf16[2,128,128]{2,1,0:T(8,128)(2,1)S(1)}, bf16[2,128,128]{2,1,0:T(8,128)(2,1)S(1)}, u32[]{:S(2)}, u32[]{:S(2)}) collective-permute-start(bf16[2,128,128]{2,1,0:T(8,128)(2,1)S(1)} %get-tuple-element.59), channel_id=1, source_target_pairs={{1,0},{2,1},{3,2},{4,3},{5,4},{6,5},{7,6},{8,7},{9,8},{10,9},{11,1... | collective-permute-start | bytes 196616 | tf_op jit(solution)/shard_map/ppermute | solution.py:21
  99.6 12.2 %collective-permute-start = (bf16[2,256,1,128]{3,1,2,0:T(8,128)(2,1)S(1)}, bf16[2,256,1,128]{3,1,2,0:T(8,128)(2,1)S(1)}, u32[]{:S(2)}, u32[]{:S(2)}) collective-permute-start(bf16[2,256,1,128]{3,1,2,0:T(8,128)(2,1)S(1)} %bitcast.347), channel_id=1, source_target_pairs={{0,1},{32,33},{64,65},{96,97},{128,129},{160,161},{192,193},{224,2... | collective-permute-start | bytes 393224 | tf_op jit(solution)/shard_map/ppermute | solution.py:34
  111.8 4.9 %collective-permute-start.1 = (bf16[2,256,1,128]{3,1,2,0:T(8,128)(2,1)S(1)}, bf16[2,256,1,128]{3,1,2,0:T(8,128)(2,1)S(1)}, u32[]{:S(2)}, u32[]{:S(2)}) collective-permute-start(bf16[2,256,1,128]{3,1,2,0:T(8,128)(2,1)S(1)} %broadcast_select_fusion.1), channel_id=1, source_target_pairs={{0,2},{1,3},{32,34},{33,35},{64,66},{65,67},{96,98},{97,99},{128,1... | collective-permute-start | bytes 393224 | tf_op jit(solution)/shard_map/ppermute | solution.py:34
  116.7 80.4 %collective-permute-start.2 = (bf16[2,256,1,128]{3,1,2,0:T(8,128)(2,1)S(1)}, bf16[2,256,1,128]{3,1,2,0:T(8,128)(2,1)S(1)}, u32[]{:S(2)}, u32[]{:S(2)}) collective-permute-start(bf16[2,256,1,128]{3,1,2,0:T(8,128)(2,1)S(1)} %broadcast_select_fusion.2), channel_id=1, source_target_pairs={{0,4},{1,5},{2,6},{3,7},{32,36},{33,37},{34,38},{35,39},{64,68},{6... | collective-permute-start | bytes 393224 | tf_op jit(solution)/shard_map/ppermute | solution.py:34
  195.3 8.1 %copy-start.6 = (bf16[2,8,384,1,128]{4,2,1,3,0:T(8,128)(2,1)}, bf16[2,8,384,1,128]{4,2,1,3,0:T(8,128)(2,1)S(1)}, u32[]{:S(2)}) copy-start(bf16[2,8,384,1,128]{4,2,1,3,0:T(8,128)(2,1)S(1)} %pad_maximum_fusion.1) | copy-start | bytes 4718596
  197.1 3.2 collective-permute-start.3
  200.3 3.3 collective-permute-start.4
  216.1 1.8 copy-start.10
  216.1 3.3 copy-start.12
  219.4 1.4 copy-start.8
  219.4 1.7 copy-start.9
  225.3 1.4 copy-start.2
  225.3 2.0 copy-start.4
  235.9 17.9 %copy-start.3 = (bf16[8,1,128,1024]{2,3,0,1:T(8,128)(2,1)S(1)}, bf16[8,1,128,1024]{2,3,0,1:T(8,128)(2,1)}, u32[]{:S(2)}) copy-start(bf16[8,1,128,1024]{2,3,0,1:T(8,128)(2,1)} %copy-done.2) | copy-start | bytes 6291460
  235.9 154.6 %all-to-all-start.8 = ((bf16[2,32,2,128,1,128]{5,2,3,0,4,1:T(2,128)(2,1)}), bf16[2,32,2,128,1,128]{5,2,3,0,4,1:T(2,128)(2,1)}, u32[]{:S(2)}, u32[]{:S(2)}) async-start(bf16[2,32,2,128,1,128]{5,2,3,0,4,1:T(2,128)(2,1)} %copy.190), calls=%async_computation.8 | async-start | bytes 8388608 | tf_op jit(solution)/shard_map/all_to_all | solution.py:198
  254.1 3.4 copy-start.5
  255.6 97.5 %collective-permute-start.9 = (f32[2,256,1,128]{3,1,2,0:T(8,128)S(1)}, f32[2,256,1,128]{3,1,2,0:T(8,128)S(1)}, u32[]{:S(2)}, u32[]{:S(2)}) collective-permute-start(f32[2,256,1,128]{3,1,2,0:T(8,128)S(1)} %pad_maximum_fusion.5), channel_id=1, source_target_pairs={{16,0},{17,1},{18,2},{19,3},{20,4},{21,5},{22,6},{23,7},{24,8},{25... | collective-permute-start | bytes 786440 | tf_op jit(solution)/shard_map/ppermute | solution.py:47
  258.2 1.1 copy-start.13
  258.2 1.7 copy-start.7
  260.6 93.9 %copy-start.11 = (bf16[1,24,128,1,128]{4,2,0,1,3:T(8,128)(2,1)S(1)}, bf16[1,24,128,1,128]{4,2,0,1,3:T(8,128)(2,1)}, u32[]{:S(2)}) copy-start(bf16[1,24,128,1,128]{4,2,0,1,3:T(8,128)(2,1)} %copy-done.10) | copy-start | bytes 2359300
  260.8 94.2 %copy-start.14 = (f32[2,10,128,1,128]{4,2,0,3,1:T(8,128)}, f32[2,10,128,1,128]{4,2,0,3,1:T(8,128)S(1)}, u32[]{:S(2)}) copy-start(f32[2,10,128,1,128]{4,2,0,3,1:T(8,128)S(1)} %bitcast_add_fusion) | copy-start | bytes 3932164
  353.2 13.8 %collective-permute-start.10 = (f32[2,256,1,128]{3,1,2,0:T(8,128)S(1)}, f32[2,256,1,128]{3,1,2,0:T(8,128)S(1)}, u32[]{:S(2)}, u32[]{:S(2)}) collective-permute-start(f32[2,256,1,128]{3,1,2,0:T(8,128)S(1)} %fusion.39), channel_id=1, source_target_pairs={{8,0},{9,1},{10,2},{11,3},{12,4},{13,5},{14,6},{15,7},{40,32},{41,... | collective-permute-start | bytes 786440 | tf_op jit(solution)/shard_map/ppermute | solution.py:47
  354.9 31.7 %collective-permute-start.7 = (bf16[2,128,1,128]{3,1,0,2:T(8,128)(2,1)S(1)}, bf16[2,128,1,128]{3,1,0,2:T(8,128)(2,1)S(1)}, u32[]{:S(2)}, u32[]{:S(2)}) collective-permute-start(bf16[2,128,1,128]{3,1,0,2:T(8,128)(2,1)S(1)} %get-tuple-element.49), channel_id=1, source_target_pairs={{0,1},{1,2},{2,3},{3,4},{4,5},{5,6},{6,7},{7,8},{8,9},{9,10},{10,1... | collective-permute-start | bytes 196616 | tf_op jit(solution)/shard_map/ppermute | solution.py:19
  359.0 27.6 %collective-permute-start.8 = (bf16[2,128,1,128]{3,1,0,2:T(8,128)(2,1)S(1)}, bf16[2,128,1,128]{3,1,0,2:T(8,128)(2,1)S(1)}, u32[]{:S(2)}, u32[]{:S(2)}) collective-permute-start(bf16[2,128,1,128]{3,1,0,2:T(8,128)(2,1)S(1)} %get-tuple-element.50), channel_id=1, source_target_pairs={{1,0},{2,1},{3,2},{4,3},{5,4},{6,5},{7,6},{8,7},{9,8},{10,9},{11,1... | collective-permute-start | bytes 196616 | tf_op jit(solution)/shard_map/ppermute | solution.py:21
  367.0 9.6 %collective-permute-start.11 = (f32[2,256,1,128]{3,1,2,0:T(8,128)S(1)}, f32[2,256,1,128]{3,1,2,0:T(8,128)S(1)}, u32[]{:S(2)}, u32[]{:S(2)}) collective-permute-start(f32[2,256,1,128]{3,1,2,0:T(8,128)S(1)} %fusion.61), channel_id=1, source_target_pairs={{4,0},{5,1},{6,2},{7,3},{36,32},{37,33},{38,34},{39,35},{68,64},{6... | collective-permute-start | bytes 786440 | tf_op jit(solution)/shard_map/ppermute | solution.py:47
  369.4 17.3 %copy-start.15 = (f32[2,10,128,1,128]{4,2,0,3,1:T(8,128)S(1)}, f32[2,10,128,1,128]{4,2,0,3,1:T(8,128)}, u32[]{:S(2)}) copy-start(f32[2,10,128,1,128]{4,2,0,3,1:T(8,128)} %copy-done.14) | copy-start | bytes 3932164
  369.4 17.3 %slice-start = ((f32[2,10,128,1,128]{4,2,0,3,1:T(8,128)}), f32[2,8,128,1,128]{4,2,0,3,1:T(8,128)S(1)}, s32[]{:S(2)}) async-start(f32[2,10,128,1,128]{4,2,0,3,1:T(8,128)} %copy-done.14), calls=%async_computation.11 | async-start | bytes 2097152 | tf_op jit(solution)/shard_map/slice | solution.py:184
  376.7 8.6 %collective-permute-start.12 = (f32[2,256,1,128]{3,1,2,0:T(8,128)S(1)}, f32[2,256,1,128]{3,1,2,0:T(8,128)S(1)}, u32[]{:S(2)}, u32[]{:S(2)}) collective-permute-start(f32[2,256,1,128]{3,1,2,0:T(8,128)S(1)} %add.165), channel_id=1, source_target_pairs={{2,0},{3,1},{34,32},{35,33},{66,64},{67,65},{98,96},{99,97},{130,1... | collective-permute-start | bytes 786440 | tf_op jit(solution)/shard_map/ppermute | solution.py:47
  385.3 15.4 %collective-permute-start.13 = (f32[2,256,1,128]{3,1,2,0:T(8,128)S(1)}, f32[2,256,1,128]{3,1,2,0:T(8,128)S(1)}, u32[]{:S(2)}, u32[]{:S(2)}) collective-permute-start(f32[2,256,1,128]{3,1,2,0:T(8,128)S(1)} %add.166), channel_id=1, source_target_pairs={{1,0},{33,32},{65,64},{97,96},{129,128},{161,160},{193,192},{225,2... | collective-permute-start | bytes 786440 | tf_op jit(solution)/shard_map/ppermute | solution.py:47
  390.5 22.1 %all-to-all-start.5 = ((bf16[16,64,128]{2,1,0:T(8,128)(2,1)}), bf16[16,64,128]{2,1,0:T(8,128)(2,1)S(1)}, u32[]{:S(2)}, u32[]{:S(2)}) async-start(bf16[16,64,128]{2,1,0:T(8,128)(2,1)} %bitcast.45), calls=%async_computation.5 | async-start | bytes 524288 | tf_op jit(solution)/shard_map/all_to_all | solution.py:220
  412.6 16.5 %all-to-all-start.7 = ((bf16[16,64,128]{2,1,0:T(8,128)(2,1)}), bf16[16,64,128]{2,1,0:T(8,128)(2,1)S(1)}, u32[]{:S(2)}, u32[]{:S(2)}) async-start(bf16[16,64,128]{2,1,0:T(8,128)(2,1)} %bitcast.67), calls=%async_computation.7 | async-start | bytes 524288 | tf_op jit(solution)/shard_map/all_to_all | solution.py:227
  420.2 39.3 %copy-start.1 = (bf16[64,2048]{1,0:T(8,128)(2,1)S(1)}, bf16[64,2048]{1,0:T(8,128)(2,1)}, u32[]{:S(2)}) copy-start(bf16[64,2048]{1,0:T(8,128)(2,1)} %param.11) | copy-start | bytes 786436
  429.0 14.6 %all-to-all-start.10 = ((bf16[16,64,128]{2,1,0:T(8,128)(2,1)}), bf16[16,64,128]{2,1,0:T(8,128)(2,1)S(1)}, u32[]{:S(2)}, u32[]{:S(2)}) async-start(bf16[16,64,128]{2,1,0:T(8,128)(2,1)} %bitcast.126), calls=%async_computation.10 | async-start | bytes 524288 | tf_op jit(solution)/shard_map/all_to_all | solution.py:235
  443.6 15.1 %all-to-all-start.9 = ((bf16[16,64,128]{2,1,0:T(8,128)(2,1)}), bf16[16,64,128]{2,1,0:T(8,128)(2,1)S(1)}, u32[]{:S(2)}, u32[]{:S(2)}) async-start(bf16[16,64,128]{2,1,0:T(8,128)(2,1)} %bitcast.124), calls=%async_computation.9 | async-start | bytes 524288 | tf_op jit(solution)/shard_map/all_to_all | solution.py:234

commit v2 on v1

--- a/solution.py
+++ b/solution.py
@@ -119,11 +119,8 @@
 def shards(queries, keys, values, grad_out, random_blocks):
     groups = lax.axis_size("seq")
     my_group = lax.axis_index("seq")
-    head_q, head_k, head_v, head_g = (
-        lax.all_to_all(queries, "head", split_axis=1, concat_axis=0, tiled=True),
-        lax.all_to_all(keys, "head", split_axis=1, concat_axis=0, tiled=True),
-        lax.all_to_all(values, "head", split_axis=1, concat_axis=0, tiled=True),
-        lax.all_to_all(grad_out, "head", split_axis=1, concat_axis=0, tiled=True),
+    head_q, head_k, head_v, head_g = lax.all_to_all(
+        jnp.stack([queries, keys, values, grad_out]), "head", split_axis=2, concat_axis=1, tiled=True
     )
     group_tokens = head_q.shape[0]
     head_count = head_q.shape[1] // HD
@@ -216,24 +213,15 @@
     total_grad = own_grad + random_sum
     grad_k = total_grad[0].reshape(group_tokens, head_count * HD).astype(jnp.bfloat16)
     grad_v = total_grad[1].reshape(group_tokens, head_count * HD).astype(jnp.bfloat16)
-    return (
-        lax.all_to_all(
-            attended.reshape(group_tokens, head_count * HD),
-            "head",
-            split_axis=0,
-            concat_axis=1,
-            tiled=True,
-        ),
-        lax.all_to_all(
-            grad_q.reshape(group_tokens, head_count * HD),
-            "head",
-            split_axis=0,
-            concat_axis=1,
-            tiled=True,
-        ),
-        lax.all_to_all(grad_k, "head", split_axis=0, concat_axis=1, tiled=True),
-        lax.all_to_all(grad_v, "head", split_axis=0, concat_axis=1, tiled=True),
-    )
+    front = lax.all_to_all(
+        jnp.stack([attended, grad_q]).reshape(2, group_tokens, head_count * HD),
+        "head",
+        split_axis=1,
+        concat_axis=2,
+        tiled=True,
+    )
+    back = lax.all_to_all(jnp.stack([grad_k, grad_v]), "head", split_axis=1, concat_axis=2, tiled=True)
+    return front[0], front[1], back[0], back[1]
 
 
 def solution(mesh):

time: 461 us -> 441 us (0.957)
  starting transfers between devices: 182 us -> 157 us
  waiting for transfers between devices: 195 us -> 179 us
  local copies, waits for them, and re-layouts: 52.9 us -> 67.8 us
    all_to_all x8 -> x3, starting transfers between devices: 41.4 us -> 20.7 us  [the longest x1 9.22 us: shards(): lax.all_to_all(jnp.stack([queries, keys, values, grad_out]), 'head', spli...]
    all_to_all x8 -> x3, waiting for transfers between devices: 62.4 us -> 48.4 us  [the longest x1 26.4 us: shards(): lax.all_to_all(jnp.stack([queries, keys, values, grad_out]), 'head', spli...]
    transpose x0 -> x5, local copies, waits for them, and re-layouts: none -> 8.36 us  [the longest x2 6.05 us: key_terms(): jnp.einsum('qhij,qihd->qjhd', window_w, rows, preferred_element_type=jnp....]
    ppermute x5, starting transfers between devices: 88.2 us -> 81.2 us  [broadcast(): got = lax.ppermute(value, axis, pairs)]
    ppermute x5, waiting for transfers between devices: 9.01 us -> 15.7 us  [broadcast(): got = lax.ppermute(value, axis, pairs)]
    unnamed x42 -> x36, local copies, waits for them, and re-layouts: 4.31 us -> 10.9 us
    ppermute x5, waiting for transfers between devices: 112 us -> 105 us  [reduce_to_first(): value = value + lax.ppermute(value, axis, pairs)]
    another operation x1 -> x6, local copies, waits for them, and re-layouts: 0.01 us -> 4.8 us  [the longest x1 1.39 us: shards(): jnp.stack([queries, keys, values, grad_out])]
  transfers between devices with their start and end apart: 25 -> 20, of which waited for: 19 -> 15; matrix products, arithmetic and copies ran while one was open for 10% -> 11% of each run, Pallas kernels for 0% -> 0%
where the time goes in v2:
time: 441 us; the launch traced here: 439 us
  waiting for transfers between devices  179 us (41%)
  starting transfers between devices  157 us (36%)
  local copies, waits for them, and re-layouts  67.8 us (15%)
  matrix products  17.5 us (4%)
  other arithmetic  16.2 us (4%)
    ppermute x5, waiting for transfers between devices, reduce_to_first(): value = value + lax.ppermute(value, axis, pairs)  105 us
    ppermute x5, starting transfers between devices, broadcast(): got = lax.ppermute(value, axis, pairs)  81.2 us
    all_to_all x1, waiting for transfers between devices, shards(): lax.all_to_all(jnp.stack([queries, keys, values, grad_out]), 'head', spli...  26.4 us
    all_to_all x1, starting transfers between devices, shards(): lax.all_to_all(outgoing.reshape(2, groups, capacity, BLK, head_count, HD)...  21.1 us
    ppermute x5, waiting for transfers between devices, broadcast(): got = lax.ppermute(value, axis, pairs)  15.7 us
    all_to_all x1, waiting for transfers between devices, shards(): lax.all_to_all(jnp.stack([grad_k, grad_v]), 'head', split_axis=1, concat_...  14.3 us
    all_to_all x1, starting transfers between devices, shards(): lax.all_to_all(request_table(random_blocks, query_count, groups, capacity...  13.7 us
    unnamed x36, local copies, waits for them, and re-layouts  10.9 us
  transfers between devices with their start and end apart: 20, of which 15 were waited for; matrix products, arithmetic and copies ran while one was open for 11% of the time, Pallas kernels for 0%

profile of v2, /device:TPU:1, one launch (start us, length us, event | category | flops | bytes accessed | tf_op | source)
XLA Modules:
  0.0 439.3 jit_solution(4418937772101540072)
XLA Ops:
  2.6 13.7 %all-to-all-start.1 = ((s32[32,1,2]{2,1,0:T(1,128)}), s32[32,1,2]{2,1,0:T(1,128)S(1)}, u32[]{:S(2)}, u32[]{:S(2)}) async-start(s32[32,1,2]{2,1,0:T(1,128)} %bitcast.21), calls=%async_computation.1 | async-start | bytes 32768 | tf_op jit(solution)/shard_map/all_to_all | solution.py:141
  16.3 1.3 pad_maximum_fusion.3
  17.7 1.4 copy.183
  19.1 2.3 reshape.1023
  21.3 3.5 all-to-all-done.1
  24.8 9.2 %all-to-all-start = ((bf16[16,2,16384]{2,1,0:T(2,128)(2,1)}), bf16[16,2,16384]{2,1,0:T(2,128)(2,1)S(1)}, u32[]{:S(2)}, u32[]{:S(2)}) async-start(bf16[16,2,16384]{2,1,0:T(2,128)(2,1)} %reshape.1023), calls=%async_computation | async-start | bytes 2097152 | tf_op jit(solution)/shard_map/all_to_all | solution.py:122
  35.6 26.4 %all-to-all-done = bf16[16,2,16384]{2,1,0:T(2,128)(2,1)S(1)} async-done(((bf16[16,2,16384]{2,1,0:T(2,128)(2,1)}), bf16[16,2,16384]{2,1,0:T(2,128)(2,1)S(1)}, u32[]{:S(2)}, u32[]{:S(2)}) %all-to-all-start) | async-done | bytes 1048608 | tf_op jit(solution)/shard_map/all_to_all | solution.py:122
  62.0 1.3 reshape.1024
  63.3 2.3 copy.184
  67.0 3.0 gather_fusion
  70.0 2.7 copy.189
  73.2 2.5 copy.190
  75.7 4.9 %all-to-all-start.2 = ((bf16[2,32,2,128,1,128]{5,3,2,0,4,1:T(8,128)(2,1)}), bf16[2,32,2,128,1,128]{5,3,2,0,4,1:T(8,128)(2,1)}, u32[]{:S(2)}, u32[]{:S(2)}) async-start(bf16[2,32,2,128,1,128]{5,3,2,0,4,1:T(8,128)(2,1)} %copy.190), calls=%async_computation.2 | async-start | bytes 8388608 | tf_op jit(solution)/shard_map/all_to_all | solution.py:150
  81.1 3.1 collective-permute-start.5
  84.1 1.3 collective-permute-start.6
  85.5 4.0 collective-permute-start
  89.5 4.8 %collective-permute-done.5 = bf16[2,128,128]{2,1,0:T(8,128)(2,1)S(1)} collective-permute-done((bf16[2,128,128]{2,1,0:T(8,128)(2,1)S(1)}, bf16[2,128,128]{2,1,0:T(8,128)(2,1)S(1)}, u32[]{:S(2)}, u32[]{:S(2)}) %collective-permute-start.5) | collective-permute-done | bytes 65568 | tf_op jit(solution)/shard_map/ppermute | solution.py:19
  94.3 2.6 collective-permute-done
  96.9 5.0 %collective-permute-start.1 = (bf16[2,256,1,128]{3,1,2,0:T(8,128)(2,1)S(1)}, bf16[2,256,1,128]{3,1,2,0:T(8,128)(2,1)S(1)}, u32[]{:S(2)}, u32[]{:S(2)}) collective-permute-start(bf16[2,256,1,128]{3,1,2,0:T(8,128)(2,1)S(1)} %broadcast_select_fusion.1), channel_id=1, source_target_pairs={{0,2},{1,3},{32,34},{33,35},{64,66},{65,67},{96,98},{97,99},{128,1... | collective-permute-start | bytes 393224 | tf_op jit(solution)/shard_map/ppermute | solution.py:34
  102.3 9.0 %collective-permute-done.1 = bf16[2,256,1,128]{3,1,2,0:T(8,128)(2,1)S(1)} collective-permute-done((bf16[2,256,1,128]{3,1,2,0:T(8,128)(2,1)S(1)}, bf16[2,256,1,128]{3,1,2,0:T(8,128)(2,1)S(1)}, u32[]{:S(2)}, u32[]{:S(2)}) %collective-permute-start.1) | collective-permute-done | bytes 131104 | tf_op jit(solution)/shard_map/ppermute | solution.py:34
  111.3 69.6 %collective-permute-start.2 = (bf16[2,256,1,128]{3,1,2,0:T(8,128)(2,1)S(1)}, bf16[2,256,1,128]{3,1,2,0:T(8,128)(2,1)S(1)}, u32[]{:S(2)}, u32[]{:S(2)}) collective-permute-start(bf16[2,256,1,128]{3,1,2,0:T(8,128)(2,1)S(1)} %broadcast_select_fusion.2), channel_id=1, source_target_pairs={{0,4},{1,5},{2,6},{3,7},{32,36},{33,37},{34,38},{35,39},{64,68},{6... | collective-permute-start | bytes 393224 | tf_op jit(solution)/shard_map/ppermute | solution.py:34
  181.0 2.4 collective-permute-done.2
  183.5 1.3 collective-permute-start.3
  185.3 1.5 collective-permute-done.3
  186.7 1.3 collective-permute-start.4
  188.0 1.6 convolution_bitcast_fusion.3
  191.3 1.6 copy.193
  194.1 4.8 %copy.191 = bf16[2,32,2,128,1,128]{5,3,2,1,0,4:T(8,128)(2,1)} copy(bf16[2,32,2,128,1,128]{5,3,2,0,4,1:T(8,128)(2,1)} %all-to-all-done.2) | data formatting | bytes 8388608 | tf_op jit(solution)/shard_map/all_to_all | solution.py:150
  198.9 4.1 gather_fusion.1
  203.0 1.6 bitcast_select_fusion
  205.8 1.4 fusion.2
  209.0 1.7 multiply_reduce_fusion
  210.6 2.7 fusion.40
  213.4 1.3 copy-done
  216.0 1.5 fusion.8
  218.5 1.4 convolution_convert_fusion
  219.8 6.7 %copy.217 = bf16[2,32,2,128,1,128]{5,2,3,0,4,1:T(2,128)(2,1)} copy(bf16[2,32,2,128,1,128]{5,2,1,3,0,4:T(2,128)(2,1)S(1)} %bitcast.269) | data formatting | bytes 8388608 | tf_op jit(solution)/shard_map/reshape | solution.py:196
  226.5 21.1 %all-to-all-start.4 = ((bf16[2,32,2,128,1,128]{5,2,3,0,4,1:T(2,128)(2,1)}), bf16[2,32,2,128,1,128]{5,2,3,0,4,1:T(2,128)(2,1)}, u32[]{:S(2)}, u32[]{:S(2)}) async-start(bf16[2,32,2,128,1,128]{5,2,3,0,4,1:T(2,128)(2,1)} %copy.217), calls=%async_computation.4 | async-start | bytes 8388608 | tf_op jit(solution)/shard_map/all_to_all | solution.py:195
  248.0 1.3 convolution_bitcast_fusion.16
  249.3 1.5 collective-permute-start.9
  250.8 1.5 convolution_bitcast_fusion
  252.4 3.0 copy.202
  255.4 2.7 convolution_bitcast_fusion.1
  258.1 3.0 copy.200
  261.2 2.1 fusion.17
  263.4 1.5 copy-done.2
  267.5 80.5 %collective-permute-done.9 = f32[2,256,1,128]{1,3,2,0:T(8,128)S(1)} collective-permute-done((f32[2,256,1,128]{1,3,2,0:T(8,128)S(1)}, f32[2,256,1,128]{1,3,2,0:T(8,128)S(1)}, u32[]{:S(2)}, u32[]{:S(2)}) %collective-permute-start.9) | collective-permute-done | bytes 262176 | tf_op jit(solution)/shard_map/ppermute | solution.py:47
  348.0 1.3 collective-permute-start.10
  349.6 16.9 %collective-permute-done.10 = f32[2,256,1,128]{1,3,2,0:T(8,128)S(1)} collective-permute-done((f32[2,256,1,128]{1,3,2,0:T(8,128)S(1)}, f32[2,256,1,128]{1,3,2,0:T(8,128)S(1)}, u32[]{:S(2)}, u32[]{:S(2)}) %collective-permute-start.10) | collective-permute-done | bytes 262176 | tf_op jit(solution)/shard_map/ppermute | solution.py:47
  366.6 1.3 collective-permute-start.11
  368.2 6.0 %collective-permute-done.11 = f32[2,256,1,128]{1,3,2,0:T(8,128)S(1)} collective-permute-done((f32[2,256,1,128]{1,3,2,0:T(8,128)S(1)}, f32[2,256,1,128]{1,3,2,0:T(8,128)S(1)}, u32[]{:S(2)}, u32[]{:S(2)}) %collective-permute-start.11) | collective-permute-done | bytes 262176 | tf_op jit(solution)/shard_map/ppermute | solution.py:47
  374.2 1.3 collective-permute-start.12
  376.4 3.1 collective-permute-start.7
  379.5 1.3 collective-permute-start.8
  380.8 2.0 pad_maximum_fusion.6
  382.9 1.3 collective-permute-start.13
  386.3 3.0 scatter-add.11
  389.3 2.1 collective-permute-done.13
  391.7 8.0 %all-to-all-start.3 = ((bf16[2,1024,128]{2,0,1:T(2,128)(2,1)}), bf16[2,1024,128]{2,0,1:T(2,128)(2,1)S(1)}, u32[]{:S(2)}, u32[]{:S(2)}) async-start(bf16[2,1024,128]{2,0,1:T(2,128)(2,1)} %pad_maximum_fusion.6), calls=%async_computation.3 | async-start | bytes 1048576 | tf_op jit(solution)/shard_map/all_to_all | solution.py:216
  400.0 7.0 %copy.218 = bf16[2,32,2,128,1,128]{5,2,1,3,0,4:T(2,128)(2,1)S(1)} copy(bf16[2,32,2,128,1,128]{5,2,3,0,4,1:T(2,128)(2,1)} %all-to-all-done.4) | data formatting | bytes 8388608 | tf_op jit(solution)/shard_map/all_to_all | solution.py:195
  407.8 1.3 copy.221
  409.1 7.7 %all-to-all-done.3 = bf16[2,1024,128]{2,0,1:T(2,128)(2,1)S(1)} async-done(((bf16[2,1024,128]{2,0,1:T(2,128)(2,1)}), bf16[2,1024,128]{2,0,1:T(2,128)(2,1)S(1)}, u32[]{:S(2)}, u32[]{:S(2)}) %all-to-all-start.3) | async-done | bytes 524320 | tf_op jit(solution)/shard_map/all_to_all | solution.py:216
  416.9 3.5 all-to-all-start.5
  423.0 14.3 %all-to-all-done.5 = bf16[2,1024,128]{2,0,1:T(2,128)(2,1)S(1)} async-done(((bf16[2,1024,128]{2,0,1:T(2,128)(2,1)}), bf16[2,1024,128]{2,0,1:T(2,128)(2,1)S(1)}, u32[]{:S(2)}, u32[]{:S(2)}) %all-to-all-start.5) | async-done | bytes 524320 | tf_op jit(solution)/shard_map/all_to_all | solution.py:223
  (129 shorter events, 27.4 us)
Async XLA Ops:
  2.6 22.2 %all-to-all-start.1 = ((s32[32,1,2]{2,1,0:T(1,128)}), s32[32,1,2]{2,1,0:T(1,128)S(1)}, u32[]{:S(2)}, u32[]{:S(2)}) async-start(s32[32,1,2]{2,1,0:T(1,128)} %bitcast.21), calls=%async_computation.1 | async-start | bytes 32768 | tf_op jit(solution)/shard_map/all_to_all | solution.py:141
  24.8 37.2 %all-to-all-start = ((bf16[16,2,16384]{2,1,0:T(2,128)(2,1)}), bf16[16,2,16384]{2,1,0:T(2,128)(2,1)S(1)}, u32[]{:S(2)}, u32[]{:S(2)}) async-start(bf16[16,2,16384]{2,1,0:T(2,128)(2,1)} %reshape.1023), calls=%async_computation | async-start | bytes 2097152 | tf_op jit(solution)/shard_map/all_to_all | solution.py:122
  75.7 118.4 %all-to-all-start.2 = ((bf16[2,32,2,128,1,128]{5,3,2,0,4,1:T(8,128)(2,1)}), bf16[2,32,2,128,1,128]{5,3,2,0,4,1:T(8,128)(2,1)}, u32[]{:S(2)}, u32[]{:S(2)}) async-start(bf16[2,32,2,128,1,128]{5,3,2,0,4,1:T(8,128)(2,1)} %copy.190), calls=%async_computation.2 | async-start | bytes 8388608 | tf_op jit(solution)/shard_map/all_to_all | solution.py:150
  81.1 13.2 %collective-permute-start.5 = (bf16[2,128,128]{2,1,0:T(8,128)(2,1)S(1)}, bf16[2,128,128]{2,1,0:T(8,128)(2,1)S(1)}, u32[]{:S(2)}, u32[]{:S(2)}) collective-permute-start(bf16[2,128,128]{2,1,0:T(8,128)(2,1)S(1)} %get-tuple-element.66), channel_id=1, source_target_pairs={{0,1},{1,2},{2,3},{3,4},{4,5},{5,6},{6,7},{7,8},{8,9},{9,10},{10,1... | collective-permute-start | bytes 196616 | tf_op jit(solution)/shard_map/ppermute | solution.py:19
  84.1 10.1 %collective-permute-start.6 = (bf16[2,128,128]{2,1,0:T(8,128)(2,1)S(1)}, bf16[2,128,128]{2,1,0:T(8,128)(2,1)S(1)}, u32[]{:S(2)}, u32[]{:S(2)}) collective-permute-start(bf16[2,128,128]{2,1,0:T(8,128)(2,1)S(1)} %get-tuple-element.67), channel_id=1, source_target_pairs={{1,0},{2,1},{3,2},{4,3},{5,4},{6,5},{7,6},{8,7},{9,8},{10,9},{11,1... | collective-permute-start | bytes 196616 | tf_op jit(solution)/shard_map/ppermute | solution.py:21
  85.5 11.5 %collective-permute-start = (bf16[2,256,1,128]{3,1,2,0:T(8,128)(2,1)S(1)}, bf16[2,256,1,128]{3,1,2,0:T(8,128)(2,1)S(1)}, u32[]{:S(2)}, u32[]{:S(2)}) collective-permute-start(bf16[2,256,1,128]{3,1,2,0:T(8,128)(2,1)S(1)} %bitcast.318), channel_id=1, source_target_pairs={{0,1},{32,33},{64,65},{96,97},{128,129},{160,161},{192,193},{224,2... | collective-permute-start | bytes 393224 | tf_op jit(solution)/shard_map/ppermute | solution.py:34
  96.9 14.3 %collective-permute-start.1 = (bf16[2,256,1,128]{3,1,2,0:T(8,128)(2,1)S(1)}, bf16[2,256,1,128]{3,1,2,0:T(8,128)(2,1)S(1)}, u32[]{:S(2)}, u32[]{:S(2)}) collective-permute-start(bf16[2,256,1,128]{3,1,2,0:T(8,128)(2,1)S(1)} %broadcast_select_fusion.1), channel_id=1, source_target_pairs={{0,2},{1,3},{32,34},{33,35},{64,66},{65,67},{96,98},{97,99},{128,1... | collective-permute-start | bytes 393224 | tf_op jit(solution)/shard_map/ppermute | solution.py:34
  111.3 72.2 %collective-permute-start.2 = (bf16[2,256,1,128]{3,1,2,0:T(8,128)(2,1)S(1)}, bf16[2,256,1,128]{3,1,2,0:T(8,128)(2,1)S(1)}, u32[]{:S(2)}, u32[]{:S(2)}) collective-permute-start(bf16[2,256,1,128]{3,1,2,0:T(8,128)(2,1)S(1)} %broadcast_select_fusion.2), channel_id=1, source_target_pairs={{0,4},{1,5},{2,6},{3,7},{32,36},{33,37},{34,38},{35,39},{64,68},{6... | collective-permute-start | bytes 393224 | tf_op jit(solution)/shard_map/ppermute | solution.py:34
  181.0 8.6 %copy-start.9 = (bf16[2,8,384,1,128]{4,2,1,3,0:T(8,128)(2,1)}, bf16[2,8,384,1,128]{4,2,1,3,0:T(8,128)(2,1)S(1)}, u32[]{:S(2)}) copy-start(bf16[2,8,384,1,128]{4,2,1,3,0:T(8,128)(2,1)S(1)} %pad_maximum_fusion.1) | copy-start | bytes 4718596
  183.5 3.2 collective-permute-start.3
  186.7 3.2 collective-permute-start.4
  204.8 1.0 copy-start.7
  204.8 2.5 copy-start.5
  207.3 1.4 copy-start.3
  207.3 1.7 copy-start.4
  213.4 1.3 copy-start
  226.5 21.2 %copy-start.1 = (bf16[8,1,128,1024]{3,2,0,1:T(8,128)(2,1)S(1)}, bf16[8,1,128,1024]{3,2,0,1:T(8,128)(2,1)}, u32[]{:S(2)}) copy-start(bf16[8,1,128,1024]{3,2,0,1:T(8,128)(2,1)} %copy-done) | copy-start | bytes 6291460
  226.5 165.2 %all-to-all-start.4 = ((bf16[2,32,2,128,1,128]{5,2,3,0,4,1:T(2,128)(2,1)}), bf16[2,32,2,128,1,128]{5,2,3,0,4,1:T(2,128)(2,1)}, u32[]{:S(2)}, u32[]{:S(2)}) async-start(bf16[2,32,2,128,1,128]{5,2,3,0,4,1:T(2,128)(2,1)} %copy.217), calls=%async_computation.4 | async-start | bytes 8388608 | tf_op jit(solution)/shard_map/all_to_all | solution.py:195
  249.3 98.7 %collective-permute-start.9 = (f32[2,256,1,128]{1,3,2,0:T(8,128)S(1)}, f32[2,256,1,128]{1,3,2,0:T(8,128)S(1)}, u32[]{:S(2)}, u32[]{:S(2)}) collective-permute-start(f32[2,256,1,128]{1,3,2,0:T(8,128)S(1)} %pad_maximum_fusion.8), channel_id=1, source_target_pairs={{16,0},{17,1},{18,2},{19,3},{20,4},{21,5},{22,6},{23,7},{24,8},{25... | collective-permute-start | bytes 786440 | tf_op jit(solution)/shard_map/ppermute | solution.py:47
  261.2 2.2 copy-start.8
  263.3 1.6 copy-start.2
  263.3 1.9 copy-start.6
  264.9 1.4 copy-start.10
  267.1 108.4 %copy-start.11 = (f32[2,10,128,1,128]{4,2,0,3,1:T(8,128)}, f32[2,10,128,1,128]{4,2,0,3,1:T(8,128)S(1)}, u32[]{:S(2)}) copy-start(f32[2,10,128,1,128]{4,2,0,3,1:T(8,128)S(1)} %bitcast_add_fusion) | copy-start | bytes 3932164
  348.0 18.5 %collective-permute-start.10 = (f32[2,256,1,128]{1,3,2,0:T(8,128)S(1)}, f32[2,256,1,128]{1,3,2,0:T(8,128)S(1)}, u32[]{:S(2)}, u32[]{:S(2)}) collective-permute-start(f32[2,256,1,128]{1,3,2,0:T(8,128)S(1)} %fusion.39), channel_id=1, source_target_pairs={{8,0},{9,1},{10,2},{11,3},{12,4},{13,5},{14,6},{15,7},{40,32},{41,... | collective-permute-start | bytes 786440 | tf_op jit(solution)/shard_map/ppermute | solution.py:47
  366.6 7.6 %collective-permute-start.11 = (f32[2,256,1,128]{1,3,2,0:T(8,128)S(1)}, f32[2,256,1,128]{1,3,2,0:T(8,128)S(1)}, u32[]{:S(2)}, u32[]{:S(2)}) collective-permute-start(f32[2,256,1,128]{1,3,2,0:T(8,128)S(1)} %fusion.64), channel_id=1, source_target_pairs={{4,0},{5,1},{6,2},{7,3},{36,32},{37,33},{38,34},{39,35},{68,64},{6... | collective-permute-start | bytes 786440 | tf_op jit(solution)/shard_map/ppermute | solution.py:47
  374.2 8.6 %collective-permute-start.12 = (f32[2,256,1,128]{1,3,2,0:T(8,128)S(1)}, f32[2,256,1,128]{1,3,2,0:T(8,128)S(1)}, u32[]{:S(2)}, u32[]{:S(2)}) collective-permute-start(f32[2,256,1,128]{1,3,2,0:T(8,128)S(1)} %add.165), channel_id=1, source_target_pairs={{2,0},{3,1},{34,32},{35,33},{66,64},{67,65},{98,96},{99,97},{130,1... | collective-permute-start | bytes 786440 | tf_op jit(solution)/shard_map/ppermute | solution.py:47
  375.6 9.9 %copy-start.12 = (f32[2,10,128,1,128]{4,2,0,3,1:T(8,128)S(1)}, f32[2,10,128,1,128]{4,2,0,3,1:T(8,128)}, u32[]{:S(2)}) copy-start(f32[2,10,128,1,128]{4,2,0,3,1:T(8,128)} %copy-done.11) | copy-start | bytes 3932164
  375.6 9.9 %slice-start = ((f32[2,10,128,1,128]{4,2,0,3,1:T(8,128)}), f32[2,8,128,1,128]{4,2,0,3,1:T(8,128)S(1)}, s32[]{:S(2)}) async-start(f32[2,10,128,1,128]{4,2,0,3,1:T(8,128)} %copy-done.11), calls=%async_computation.6 | async-start | bytes 2097152 | tf_op jit(solution)/shard_map/slice | solution.py:181
  376.4 7.8 %collective-permute-start.7 = (bf16[2,128,1,128]{3,1,0,2:T(8,128)(2,1)S(1)}, bf16[2,128,1,128]{3,1,0,2:T(8,128)(2,1)S(1)}, u32[]{:S(2)}, u32[]{:S(2)}) collective-permute-start(bf16[2,128,1,128]{3,1,0,2:T(8,128)(2,1)S(1)} %get-tuple-element.49), channel_id=1, source_target_pairs={{0,1},{1,2},{2,3},{3,4},{4,5},{5,6},{6,7},{7,8},{8,9},{9,10},{10,1... | collective-permute-start | bytes 196616 | tf_op jit(solution)/shard_map/ppermute | solution.py:19
  379.5 6.0 %collective-permute-start.8 = (bf16[2,128,1,128]{3,1,0,2:T(8,128)(2,1)S(1)}, bf16[2,128,1,128]{3,1,0,2:T(8,128)(2,1)S(1)}, u32[]{:S(2)}, u32[]{:S(2)}) collective-permute-start(bf16[2,128,1,128]{3,1,0,2:T(8,128)(2,1)S(1)} %get-tuple-element.50), channel_id=1, source_target_pairs={{1,0},{2,1},{3,2},{4,3},{5,4},{6,5},{7,6},{8,7},{9,8},{10,9},{11,1... | collective-permute-start | bytes 196616 | tf_op jit(solution)/shard_map/ppermute | solution.py:21
  382.9 8.5 %collective-permute-start.13 = (f32[2,256,1,128]{1,3,2,0:T(8,128)S(1)}, f32[2,256,1,128]{1,3,2,0:T(8,128)S(1)}, u32[]{:S(2)}, u32[]{:S(2)}) collective-permute-start(f32[2,256,1,128]{1,3,2,0:T(8,128)S(1)} %add.166), channel_id=1, source_target_pairs={{1,0},{33,32},{65,64},{97,96},{129,128},{161,160},{193,192},{225,2... | collective-permute-start | bytes 786440 | tf_op jit(solution)/shard_map/ppermute | solution.py:47
  391.7 25.2 %all-to-all-start.3 = ((bf16[2,1024,128]{2,0,1:T(2,128)(2,1)}), bf16[2,1024,128]{2,0,1:T(2,128)(2,1)S(1)}, u32[]{:S(2)}, u32[]{:S(2)}) async-start(bf16[2,1024,128]{2,0,1:T(2,128)(2,1)} %pad_maximum_fusion.6), calls=%async_computation.3 | async-start | bytes 1048576 | tf_op jit(solution)/shard_map/all_to_all | solution.py:216
  416.9 20.4 %all-to-all-start.5 = ((bf16[2,1024,128]{2,0,1:T(2,128)(2,1)}), bf16[2,1024,128]{2,0,1:T(2,128)(2,1)S(1)}, u32[]{:S(2)}, u32[]{:S(2)}) async-start(bf16[2,1024,128]{2,0,1:T(2,128)(2,1)} %copy.221), calls=%async_computation.5 | async-start | bytes 1048576 | tf_op jit(solution)/shard_map/all_to_all | solution.py:223
